TPU v7x, 128 devices: a whole 4x4x4 slice. The times are simulated.
128 devices in a mesh: prow: 8 (over z, core), pcol: 16 (over x, y).
Axes of the slice: x: 4, y: 4, z: 4, core: 2. Of those that a mesh axis runs over, the one named last changes fastest.
Arguments:
- front: float32 [4, 8, 512, 2, 16, 512], P(None, 'prow', None, None, 'pcol'), as said below
- child_block: float32 [2, 8, 512, 1, 16, 512], P(None, 'prow', None, None, 'pcol'), as said below
- child_to_parent: int32 [8192], replicated, may hold values from 0 to 16383, as said below
Outputs:
- front_out: float32 [4, 8, 512, 2, 16, 512], P(None, 'prow', None, None, 'pcol')
Inputs may be any that keep to these rules, and one draw needn't show every extreme that they name: `child_to_parent`: all entries are distinct. Child indices come in groups of 32 consecutive positions of one grid row's local order that share a destination. The child indices held by one grid row (row blocks congruent to it modulo 8) send at most 256 of them to the parent row blocks of any one grid row, and those held by one grid column at most 64 to the parent column blocks of any one grid column; both bounds are reached in every draw. `front`: Symmetric. `child_block`: Symmetric.
All inputs are finite; a program needn't handle non-finite values.
Results may differ from a plain program's by a relative error of at most 0.0001.
Values sent between devices are 32-bit elements; how exact they have to be, the bound alone decides.
No kernel may reach another device: no remote copies, remote signals or barrier semaphores. Data moves between devices by JAX's collectives and lax.ppermute only.
A program may use at most 192 MiB of HBM per device.

v0:
```python
import jax
import jax.numpy as jnp
from jax import lax
from jax.sharding import PartitionSpec as P

NP = 2


HIGHEST = lax.Precision.HIGHEST


def from_root(x, axis, root):
    mine = lax.axis_index(axis) == root
    return lax.psum(jnp.where(mine, x, jnp.zeros_like(x)), axis)


def slot_ranks(destiny, groups):
    one_hot = (destiny[:, :, None] == jnp.arange(groups, dtype=jnp.int32)[None, None, :]).astype(
        jnp.int32
    )
    return jnp.sum(jnp.cumsum(one_hot, axis=1) * one_hot, axis=2) - 1


def by_source(values, blocks_local, groups, block_width):
    return jnp.transpose(values.reshape(blocks_local, groups, block_width), (1, 0, 2)).reshape(
        groups, blocks_local * block_width
    )


def route_tables(mapping, blocks_local, groups, block_width, my_index, capacity, parent_len):
    local_len = blocks_local * block_width
    parent_blk = mapping // block_width
    dest_group = by_source(parent_blk % groups, blocks_local, groups, block_width)
    parent_pos = by_source(
        parent_blk // groups * block_width + mapping % block_width,
        blocks_local,
        groups,
        block_width,
    )
    slot_rank = slot_ranks(dest_group, groups)
    own_dest = lax.dynamic_index_in_dim(dest_group, my_index, 0, keepdims=False)
    own_slot = lax.dynamic_index_in_dim(slot_rank, my_index, 0, keepdims=False)
    send_pick = (
        jnp.full((groups * capacity,), local_len, jnp.int32)
        .at[own_dest * capacity + own_slot]
        .set(jnp.arange(local_len, dtype=jnp.int32))
    )
    flat_slot = jnp.arange(groups, dtype=jnp.int32)[:, None] * capacity + slot_rank
    landing = jnp.where(dest_group == my_index, parent_pos, parent_len)
    recv_pick = (
        jnp.full((parent_len,), groups * capacity, jnp.int32)
        .at[landing.reshape(-1)]
        .set(flat_slot.reshape(-1), mode="drop")
    )
    return (send_pick, recv_pick)


def factor_block(block_in, tile_size):
    order_len = block_in.shape[0]
    num_tiles = order_len // tile_size
    identity = jnp.eye(tile_size, dtype=jnp.float32)
    zero_tile = jnp.zeros((tile_size, tile_size), jnp.float32)
    low_tiles = [[zero_tile for col_tile in range(num_tiles)] for row_tile in range(num_tiles)]
    diag_inverses = []
    working = block_in
    for col_tile in range(num_tiles):
        tile_start = col_tile * tile_size
        tile_end = tile_start + tile_size
        diag_tile = jnp.linalg.cholesky(working[tile_start:tile_end, tile_start:tile_end])
        diag_inverse = jax.scipy.linalg.solve_triangular(diag_tile, identity, lower=True)
        low_tiles[col_tile][col_tile] = diag_tile
        diag_inverses.append(diag_inverse)
        if tile_end < order_len:
            stripe_rows = jnp.dot(
                working[tile_end:, tile_start:tile_end], diag_inverse.T, precision=HIGHEST
            )
            for row_tile in range(col_tile + 1, num_tiles):
                offset = (row_tile - col_tile - 1) * tile_size
                low_tiles[row_tile][col_tile] = stripe_rows[offset : offset + tile_size]
            working = working.at[tile_end:, tile_end:].add(
                -jnp.dot(stripe_rows, stripe_rows.T, precision=HIGHEST)
            )
    inv_tiles = [[zero_tile for col_tile in range(num_tiles)] for row_tile in range(num_tiles)]
    for row_tile in range(num_tiles):
        inv_tiles[row_tile][row_tile] = diag_inverses[row_tile]
        for col_tile in range(row_tile - 1, -1, -1):
            partial_sum = zero_tile
            for mid_tile in range(col_tile, row_tile):
                partial_sum = partial_sum + jnp.dot(
                    low_tiles[row_tile][mid_tile], inv_tiles[mid_tile][col_tile], precision=HIGHEST
                )
            inv_tiles[row_tile][col_tile] = -jnp.dot(
                diag_inverses[row_tile], partial_sum, precision=HIGHEST
            )
    return (jnp.block(low_tiles), jnp.block(inv_tiles))


def local(front, child_block, child_to_parent):
    grid_rows = lax.axis_size("prow")
    grid_cols = lax.axis_size("pcol")
    my_row = lax.axis_index("prow")
    my_col = lax.axis_index("pcol")
    row_blocks = front.shape[0]
    block_width = front.shape[2]
    col_blocks = front.shape[3]
    child_rblocks = child_block.shape[0]
    child_cblocks = child_block.shape[3]
    local_rows = row_blocks * block_width
    local_cols = col_blocks * block_width
    child_rows = child_rblocks * block_width
    child_cols = child_cblocks * block_width
    cap_rows = 2 * child_rows // grid_rows
    cap_cols = 2 * child_cols // grid_cols
    tile_size = min(64, block_width)
    row_send, row_recv = route_tables(
        child_to_parent, child_rblocks, grid_rows, block_width, my_row, cap_rows, local_rows
    )
    col_send, col_recv = route_tables(
        child_to_parent, child_cblocks, grid_cols, block_width, my_col, cap_cols, local_cols
    )
    padded = jnp.pad(child_block.reshape(child_rows, child_cols), ((0, 1), (0, 1)))
    moved = jnp.take(jnp.take(padded, row_send, axis=0), col_send, axis=1).reshape(
        grid_rows, cap_rows, grid_cols, cap_cols
    )
    moved = lax.all_to_all(
        lax.all_to_all(moved, "prow", split_axis=0, concat_axis=0, tiled=True),
        "pcol",
        split_axis=2,
        concat_axis=2,
        tiled=True,
    )
    arrived = jnp.pad(moved.reshape(grid_rows * cap_rows, grid_cols * cap_cols), ((0, 1), (0, 1)))
    added = jnp.take(jnp.take(arrived, row_recv, axis=0), col_recv, axis=1)
    matrix = front.reshape(local_rows, local_cols) + added
    row_ids = jnp.repeat(jnp.arange(row_blocks, dtype=jnp.int32) * grid_rows + my_row, block_width)
    col_ids = jnp.repeat(jnp.arange(col_blocks, dtype=jnp.int32) * grid_cols + my_col, block_width)
    stride = grid_cols // grid_rows
    pick_blocks = my_col // grid_rows + jnp.arange(col_blocks, dtype=jnp.int32) * stride
    for panel_id in range(NP):
        row_home = panel_id % grid_rows
        col_home = panel_id % grid_cols
        row_local = panel_id // grid_rows * block_width
        col_local = panel_id // grid_cols * block_width
        candidate = matrix[row_local : row_local + block_width, col_local : col_local + block_width]
        diagonal = from_root(candidate, "prow", row_home)
        column = matrix[:, col_local : col_local + block_width]
        is_owner = my_col == col_home

        def factor_panel(operands):
            block_in, column_in = operands
            low_factor, low_inverse = factor_block(block_in, tile_size)
            solved = jnp.dot(column_in, low_inverse.T, precision=HIGHEST)
            solved = jnp.where((row_ids > panel_id)[:, None], solved, 0.0)
            current = solved[row_local : row_local + block_width]
            return solved.at[row_local : row_local + block_width].set(
                jnp.where(my_row == row_home, low_factor, current)
            )

        def skip_panel(operands):
            return jnp.zeros_like(operands[1])

        panel_block = lax.cond(is_owner, factor_panel, skip_panel, (diagonal, column))
        rows_panel = from_root(panel_block, "pcol", col_home)
        chosen = jnp.take(
            rows_panel.reshape(row_blocks, block_width, block_width), pick_blocks, axis=0
        ).reshape(local_cols, block_width)
        cols_panel = from_root(chosen, "prow", my_col % grid_rows)
        row_factor = jnp.where((row_ids > panel_id)[:, None], rows_panel, 0.0)
        col_factor = jnp.where((col_ids > panel_id)[:, None], cols_panel, 0.0)
        matrix = matrix - jnp.dot(row_factor, col_factor.T, precision=HIGHEST)
        kept = matrix[:, col_local : col_local + block_width]
        matrix = matrix.at[:, col_local : col_local + block_width].set(
            jnp.where(is_owner, rows_panel, kept)
        )
    return matrix.reshape(front.shape)


def solution(mesh):
    in_specs = (
        P(None, "prow", None, None, "pcol", None),
        P(None, "prow", None, None, "pcol", None),
        P(),
    )
    out_specs = P(None, "prow", None, None, "pcol", None)
    return jax.shard_map(local, mesh=mesh, in_specs=in_specs, out_specs=out_specs, check_vma=False)
```

profile of v0, /device:TPU:1, one launch (start us, length us, event | category | flops | bytes accessed | tf_op | source)
XLA Modules:
  0.0 1307.7 jit_solution(4032079716656100237)
XLA Ops:
  7.7 18.0 %reduce-window.16 = s32[8,8,8,128]{3,2,1,0:T(8,128)S(1)} reduce-window(s32[8,8,8,128]{3,2,1,0:T(8,128)S(1)} %fusion.351, s32[]{:T(128)} %constant.712.clone.1), window={size=1x1x1x128 pad=0_0x0_0x0_0x127_0}, to_apply=%region_4.5 | reduce-window | flops 8323072 | bytes 524292 | tf_op jit(solution)/shard_map/reduce-window.2
  33.0 18.1 %reduce-window.14 = s32[16,16,4,128]{3,1,2,0:T(8,128)S(1)} reduce-window(s32[16,16,4,128]{3,1,2,0:T(8,128)S(1)} %fusion.349, s32[]{:T(128)} %constant.712.clone.1), window={size=1x1x1x128 pad=0_0x0_0x0_0x127_0}, to_apply=%region_0.1 | reduce-window | flops 16646144 | bytes 1048580 | tf_op jit(solution)/shard_map/reduce-window
  74.7 11.1 gather_fusion.1
  96.6 100.2 %all_to_all.10 = f32[8,256,16,64]{1,3,2,0:T(8,128)S(1)} all-to-all(f32[8,256,16,64]{1,3,2,0:T(8,128)S(1)} %copy_select_fusion), channel_id=1, replica_groups=mesh['prow'=8,'pcol'=16] {'prow'}, dimensions={0} | all-to-all | bytes 16777216 | tf_op jit(solution)/shard_map/all_to_all | solution.py:126
  207.9 29.2 %reduce.45 = f32[4,512,2,512]{3,2,1,0:T(2,128)} reduce(f32[4,1,512,2,1,512]{5,4,3,2,1,0:T(1,128)} %param.112, f32[]{:T(128)} %constant.742), dimensions={1,4}, to_apply=%param.112.reduce_sub_computation | reduce | bytes 16777220 | tf_op args[0]
  245.8 30.4 %scatter_custom_fusion = s32[1024]{0:T(1024)S(1)} fusion(s32[8192]{0:T(1024)S(1)} %get-tuple-element.401, s32[8192]{0:T(1024)S(1)} %bitcast.594, s32[]{:T(128)} %constant.710.clone.1), kind=kCustom, calls=%fused_computation.737 | custom fusion | bytes 4100 | tf_op jit(solution)/shard_map/scatter | solution.py:53
  276.3 30.9 %scatter_custom_fusion.1 = s32[2048]{0:T(1024)S(1)} fusion(s32[8192]{0:T(1024)S(1)} %bitcast.595, s32[8192]{0:T(1024)S(1)} %bitcast.593, s32[]{:T(128)} %constant.723.clone.1), kind=kCustom, calls=%fused_computation.728 | custom fusion | bytes 8196 | tf_op jit(solution)/shard_map/scatter | solution.py:53
  307.2 41.8 %all-to-all-done.1 = f32[8,256,16,64]{1,3,0,2:T(8,128)} async-done(((f32[8,256,16,64]{1,3,0,2:T(8,128)}), f32[8,256,16,64]{1,3,0,2:T(8,128)}, u32[]{:S(2)}, u32[]{:S(2)}) %all-to-all-start.1) | async-done | bytes 8388640 | tf_op jit(solution)/shard_map/all_to_all | solution.py:125
  349.0 14.5 %copy.388 = f32[8,256,16,64]{3,2,1,0:T(8,128)} copy(f32[8,256,16,64]{1,3,0,2:T(8,128)} %all-to-all-done.1) | data formatting | bytes 16777216 | tf_op jit(solution)/shard_map/reshape | solution.py:132
  363.6 14.5 %reshape.848 = f32[2048,1024]{1,0:T(8,128)} reshape(f32[8,256,16,64]{3,2,1,0:T(8,128)} %copy.388) | data formatting | bytes 16777216 | tf_op jit(solution)/shard_map/reshape | solution.py:132
  386.1 16.1 %gather_fusion.2 = f32[2048,1025]{1,0:T(8,128)} fusion(f32[2049,1025]{1,0:T(8,128)} %pad.87, s32[2048]{0:T(1024)S(1)} %fusion.363), kind=kCustom, calls=%fused_computation.4 | custom fusion | bytes 16801792 | tf_op jit(solution)/shard_map/jit(_take)/gather | solution.py:133
  419.7 12.3 gather_fusion.3
  441.2 12.2 bitcast_add_fusion.16
  455.9 68.7 %all-reduce.9.cloned.1.call-done = f32[512,512]{1,0:T(8,128)} async-done(((f32[512,512]{1,0:T(8,128)}), f32[512,512]{1,0:T(8,128)}) %all-reduce.9.cloned.1.call-update) | async-done | bytes 1048592 | tf_op jit(solution)/shard_map/psum | solution.py:14
  524.6 150.1 %conditional.2 = (f32[2048,512]{1,0:T(8,128)}) conditional(s32[]{:T(128)} %convert_element_type.56, () %tuple.93, (s32[2048]{0:T(1024)S(1)}, f32[512,512]{1,0:T(8,128)}, f32[2048,1024]{1,0:T(8,128)}, s32[]{:T(128)}) %tuple.203), branch_computations={%region_11.12_spmd, %region_12.18_spmd} | conditional | flops 7351585280 | bytes 43057184 | solution.py:162
  662.1 9.9 select_bitcast_fusion
  679.6 99.3 %all-reduce.11.cloned.1.call-done = f32[2048,512]{1,0:T(8,128)} async-done(((f32[2048,512]{1,0:T(8,128)}), f32[2048,512]{1,0:T(8,128)}) %all-reduce.11.cloned.1.call-update) | async-done | bytes 4194320 | tf_op jit(solution)/shard_map/psum | solution.py:14
  784.3 63.6 %all-reduce.13.cloned.1.call-done = f32[1024,512]{1,0:T(8,128)} async-done(((f32[1024,512]{1,0:T(8,128)}), f32[1024,512]{1,0:T(8,128)}) %all-reduce.13.cloned.1.call-update) | async-done | bytes 2097168 | tf_op jit(solution)/shard_map/psum | solution.py:14
  847.9 19.5 %fusion.331 = f32[2048,1024]{1,0:T(8,128)} fusion(f32[2048,1024]{1,0:T(8,128)} %bitcast_add_fusion.16, f32[2048,512]{1,0:T(8,128)} %all-reduce.11.cloned.1.call-done, f32[1024,512]{1,0:T(8,128)} %all-reduce.13.cloned.1.call-done, pred[2048]{0:T(1024)(128)(4,1)S(1)} %get-tuple-element.408, pred[1024]{0:T(1024)(128)(4,1)S(1)} %gt.47), kind=kOutput, calls=%fused_computation.644 | convolution fusion | flops 12888571904 | bytes 23071744 | tf_op jit(solution)/shard_map/dot_general | solution.py:170
  874.4 62.4 %all-reduce.15.cloned.1.call-done = f32[512,512]{1,0:T(8,128)} async-done(((f32[512,512]{1,0:T(8,128)}), f32[512,512]{1,0:T(8,128)}) %all-reduce.15.cloned.1.call-update) | async-done | bytes 1048592 | tf_op jit(solution)/shard_map/psum | solution.py:14
  947.9 244.9 %all-reduce.17.cloned.1.call-done = f32[2048,512]{1,0:T(8,128)} async-done(((f32[2048,512]{1,0:T(8,128)}), f32[2048,512]{1,0:T(8,128)}) %all-reduce.17.cloned.1.call-update) | async-done | bytes 4194320 | tf_op jit(solution)/shard_map/psum | solution.py:14
  1197.6 64.3 %all-reduce.19.cloned.1.call-done = f32[1024,512]{1,0:T(8,128)} async-done(((f32[1024,512]{1,0:T(8,128)}), f32[1024,512]{1,0:T(8,128)}) %all-reduce.19.cloned.1.call-update) | async-done | bytes 2097168 | tf_op jit(solution)/shard_map/psum | solution.py:14
  1261.9 19.4 %fusion.334 = f32[2048,1024]{1,0:T(8,128)} fusion(f32[2048,1024]{1,0:T(8,128)} %get-tuple-element.329, f32[2048,512]{1,0:T(8,128)} %all-reduce.17.cloned.1.call-done, f32[1024,512]{1,0:T(8,128)} %all-reduce.19.cloned.1.call-done, pred[2048]{0:T(1024)(128)(4,1)S(1)} %get-tuple-element.407, pred[1024]{0:T(1024)(128)(4,1)S(1)} %gt.51), kind=kOutput, calls=%fused_computation.645 | convolution fusion | flops 12888571904 | bytes 23071744 | tf_op jit(solution)/shard_map/dot_general | solution.py:170
  1287.1 13.5 %reshape.849 = f32[4,1,512,2,1,512]{5,4,3,2,1,0:T(1,128)} reshape(f32[2048,1024]{1,0:T(8,128)} %fusion.326) | data formatting | bytes 16777216 | tf_op jit(solution)/shard_map/reshape | solution.py:175
  (360 shorter events, 279.3 us)
Async XLA Ops:
  6.5 48.5 %copy-start.2 = (f32[2,1,512,1,1,512]{5,4,3,2,1,0:T(1,128)S(1)}, f32[2,1,512,1,1,512]{5,4,3,2,1,0:T(1,128)}, u32[]{:S(2)}) copy-start(f32[2,1,512,1,1,512]{5,4,3,2,1,0:T(1,128)} %param.113) | copy-start | bytes 6291460
  200.6 148.5 %all-to-all-start.1 = ((f32[8,256,16,64]{1,3,0,2:T(8,128)}), f32[8,256,16,64]{1,3,0,2:T(8,128)}, u32[]{:S(2)}, u32[]{:S(2)}) async-start(f32[8,256,16,64]{1,3,0,2:T(8,128)} %copy.374), calls=%async_computation.1 | async-start | bytes 16777216 | tf_op jit(solution)/shard_map/all_to_all | solution.py:125
  207.5 317.1 %all-reduce.9.cloned.1.call-start = ((), (), s32[]{:S(2)}) async-start(), calls=%async_computation.2 | async-start | bytes 2097152 | tf_op jit(solution)/shard_map/psum | solution.py:14
  455.8 323.1 %all-reduce.11.cloned.1.call-start = ((), (), s32[]{:S(2)}) async-start(), calls=%async_computation.3 | async-start | bytes 8388608 | tf_op jit(solution)/shard_map/psum | solution.py:14
  679.4 168.5 %all-reduce.13.cloned.1.call-start = ((), (), s32[]{:S(2)}) async-start(), calls=%async_computation.4 | async-start | bytes 4194304 | tf_op jit(solution)/shard_map/psum | solution.py:14
  783.5 153.2 %all-reduce.15.cloned.1.call-start = ((), (), s32[]{:S(2)}) async-start(), calls=%async_computation.5 | async-start | bytes 2097152 | tf_op jit(solution)/shard_map/psum | solution.py:14
  847.9 19.5 %copy-start.1 = (f32[2048,512]{1,0:T(8,128)S(1)}, f32[2048,512]{1,0:T(8,128)}, u32[]{:S(2)}) copy-start(f32[2048,512]{1,0:T(8,128)} %all-reduce.11.cloned.1.call-done) | copy-start | bytes 12582916
  874.3 318.6 %all-reduce.17.cloned.1.call-start = ((), (), s32[]{:S(2)}) async-start(), calls=%async_computation.6 | async-start | bytes 8388608 | tf_op jit(solution)/shard_map/psum | solution.py:14
  947.9 314.0 %all-reduce.19.cloned.1.call-start = ((), (), s32[]{:S(2)}) async-start(), calls=%async_computation.7 | async-start | bytes 4194304 | tf_op jit(solution)/shard_map/psum | solution.py:14
  1261.9 19.4 %copy-start = (f32[2048,512]{1,0:T(8,128)S(1)}, f32[2048,512]{1,0:T(8,128)}, u32[]{:S(2)}) copy-start(f32[2048,512]{1,0:T(8,128)} %all-reduce.17.cloned.1.call-done) | copy-start | bytes 12582916
Sparse Core Ops, SparseCore 0:
  455.9 68.6 all-reduce.8
  679.6 99.2 all-reduce.10
  783.7 64.2 all-reduce.12
  874.4 62.2 all-reduce.14
  948.0 244.8 all-reduce.16
  1197.6 64.2 all-reduce.18
where the time goes:
time: 1310 us
  waiting for transfers between devices  645 us (49%)
  local copies, waits for them, and re-layouts  229 us (17%)
  other arithmetic  222 us (17%)
  blocking collectives  100 us (8%)
  matrix products  81.8 us (6%)
  between operations  14.2 us (1%)
    psum x6, waiting for transfers between devices, from_root(): return lax.psum(jnp.where(mine, x, jnp.zeros_like(x)), axis)  603 us
    all_to_all x1, blocking collectives, local(): lax.all_to_all(moved, 'prow', split_axis=0, concat_axis=0, tiled=True)  100 us
    scatter x2, local copies, waits for them, and re-layouts, route_tables(): recv_pick = jnp.full((parent_len,), groups * capacity, jnp.int32).at[land...  61.3 us
    another operation x24, other arithmetic, factor_block(): jnp.linalg.cholesky(working[tile_start:tile_end, tile_start:tile_end])  52.7 us
    another operation x16, other arithmetic, factor_block(): jax.scipy.linalg.solve_triangular(diag_tile, identity, lower=True)  43.7 us
    all_to_all x1, waiting for transfers between devices, local(): lax.all_to_all(lax.all_to_all(moved, 'prow', split_axis=0, concat_axis=0,...  41.8 us
    dot_general x2, matrix products, local(): matrix = matrix - jnp.dot(row_factor, col_factor.T, precision=HIGHEST)  38.9 us
    another operation x6, other arithmetic  38.3 us
  transfers between devices with their start and end apart: 7, of which 7 were waited for; matrix products, arithmetic and copies ran while one was open for 8% of the time, Pallas kernels for 0%

commit v1 on v0

--- a/solution.py
+++ b/solution.py
@@ -132,46 +132,59 @@
     arrived = jnp.pad(moved.reshape(grid_rows * cap_rows, grid_cols * cap_cols), ((0, 1), (0, 1)))
     added = jnp.take(jnp.take(arrived, row_recv, axis=0), col_recv, axis=1)
     matrix = front.reshape(local_rows, local_cols) + added
-    row_ids = jnp.repeat(jnp.arange(row_blocks, dtype=jnp.int32) * grid_rows + my_row, block_width)
-    col_ids = jnp.repeat(jnp.arange(col_blocks, dtype=jnp.int32) * grid_cols + my_col, block_width)
-    stride = grid_cols // grid_rows
-    pick_blocks = my_col // grid_rows + jnp.arange(col_blocks, dtype=jnp.int32) * stride
-    for panel_id in range(NP):
-        row_home = panel_id % grid_rows
-        col_home = panel_id % grid_cols
-        row_local = panel_id // grid_rows * block_width
-        col_local = panel_id // grid_cols * block_width
-        candidate = matrix[row_local : row_local + block_width, col_local : col_local + block_width]
-        diagonal = from_root(candidate, "prow", row_home)
-        column = matrix[:, col_local : col_local + block_width]
-        is_owner = my_col == col_home
-
-        def factor_panel(operands):
-            block_in, column_in = operands
-            low_factor, low_inverse = factor_block(block_in, tile_size)
-            solved = jnp.dot(column_in, low_inverse.T, precision=HIGHEST)
-            solved = jnp.where((row_ids > panel_id)[:, None], solved, 0.0)
-            current = solved[row_local : row_local + block_width]
-            return solved.at[row_local : row_local + block_width].set(
-                jnp.where(my_row == row_home, low_factor, current)
+    panel = NP * block_width
+    row_blk = jnp.repeat(jnp.arange(row_blocks, dtype=jnp.int32) * grid_rows + my_row, block_width)
+    col_blk = jnp.repeat(jnp.arange(col_blocks, dtype=jnp.int32) * grid_cols + my_col, block_width)
+    first_cols = matrix[:, :block_width]
+    first_rows = matrix[:block_width, :]
+    zero_cols = jnp.zeros_like(first_cols)
+    zero_rows = jnp.zeros_like(first_rows)
+    x_part = jnp.concatenate(
+        [jnp.where(my_col == p, first_cols, zero_cols) for p in range(NP)], axis=1
+    )
+    y_part = jnp.concatenate(
+        [jnp.where(my_row == p, first_rows, zero_rows) for p in range(NP)], axis=0
+    )
+    corner = first_rows[:, :block_width]
+    zero_corner = jnp.zeros_like(corner)
+    d_part = jnp.concatenate(
+        [
+            jnp.concatenate(
+                [
+                    jnp.where((my_row == p) & (my_col == q), corner, zero_corner)
+                    for q in range(NP)
+                ],
+                axis=1,
             )
-
-        def skip_panel(operands):
-            return jnp.zeros_like(operands[1])
-
-        panel_block = lax.cond(is_owner, factor_panel, skip_panel, (diagonal, column))
-        rows_panel = from_root(panel_block, "pcol", col_home)
-        chosen = jnp.take(
-            rows_panel.reshape(row_blocks, block_width, block_width), pick_blocks, axis=0
-        ).reshape(local_cols, block_width)
-        cols_panel = from_root(chosen, "prow", my_col % grid_rows)
-        row_factor = jnp.where((row_ids > panel_id)[:, None], rows_panel, 0.0)
-        col_factor = jnp.where((col_ids > panel_id)[:, None], cols_panel, 0.0)
-        matrix = matrix - jnp.dot(row_factor, col_factor.T, precision=HIGHEST)
-        kept = matrix[:, col_local : col_local + block_width]
-        matrix = matrix.at[:, col_local : col_local + block_width].set(
-            jnp.where(is_owner, rows_panel, kept)
+            for p in range(NP)
+        ],
+        axis=0,
+    )
+    x_full = lax.psum(x_part, "pcol")
+    y_full = lax.psum(y_part, "prow")
+    d_full = lax.psum(d_part, ("prow", "pcol"))
+    low = jnp.tril(jnp.linalg.cholesky(d_full))
+    low_inv = jax.scipy.linalg.solve_triangular(
+        low, jnp.eye(panel, dtype=jnp.float32), lower=True
+    )
+    rows_f = jnp.dot(x_full, low_inv.T, precision=HIGHEST)
+    cols_f = lax.dot_general(
+        y_full, low_inv, (((0,), (1,)), ((), ())), precision=HIGHEST
+    )
+    low_rows = lax.dynamic_slice_in_dim(low, jnp.minimum(my_row, NP - 1) * block_width, block_width, 0)
+    head = jnp.where(my_row < NP, low_rows, rows_f[:block_width])
+    rows_f = jnp.concatenate([head, rows_f[block_width:]], axis=0)
+    lane = jnp.arange(panel, dtype=jnp.int32)[None, :]
+    keep_row = (row_blk[:, None] >= NP) | (lane < (row_blk[:, None] * block_width))
+    rows_u = jnp.where(keep_row, rows_f, 0.0)
+    cols_u = jnp.where((col_blk >= NP)[:, None], cols_f, 0.0)
+    matrix = matrix - jnp.dot(rows_u, cols_u.T, precision=HIGHEST)
+    out_first = matrix[:, :block_width]
+    for p in range(NP):
+        out_first = jnp.where(
+            my_col == p, rows_f[:, p * block_width : (p + 1) * block_width], out_first
         )
+    matrix = jnp.concatenate([out_first, matrix[:, block_width:]], axis=1)
     return matrix.reshape(front.shape)
 
 

time: 1310 us -> 1180 us (0.901)
  waiting for transfers between devices: 645 us -> 242 us
  other arithmetic: 222 us -> 379 us
  matrix products: 81.8 us -> 138 us
  local copies, waits for them, and re-layouts: 229 us -> 281 us
    psum x6 -> x3, waiting for transfers between devices: 603 us -> 148 us  [the longest x1 148 us: local(): d_full = lax.psum(d_part, ('prow', 'pcol'))]
    another operation x46 -> x39, other arithmetic: 135 us -> 291 us  [the longest x31 168 us: local(): low = jnp.tril(jnp.linalg.cholesky(d_full))]
    another operation x8 -> x29, matrix products: 2.02 us -> 56 us  [the longest x15 28.5 us: local(): jax.scipy.linalg.solve_triangular(low, jnp.eye(panel, dtype=jnp.float32),...]
    all_to_all x1, waiting for transfers between devices: 41.8 us -> 94 us  [local(): lax.all_to_all(lax.all_to_all(moved, 'prow', split_axis=0, concat_axis=0,...]
    another operation x9 -> x72, local copies, waits for them, and re-layouts: 5.98 us -> 34 us
    reshape x1 -> x2, local copies, waits for them, and re-layouts: 13.5 us -> 31.3 us  [local(): return matrix.reshape(front.shape)]
    scatter x3 -> x0, other arithmetic: 14 us -> none  [the longest x2 11.6 us: local(): matrix.at[:, col_local:col_local + block_width]]
    unnamed x13 -> x21, local copies, waits for them, and re-layouts: 16.4 us -> 27.5 us
  transfers between devices with their start and end apart: 7 -> 4, of which waited for: 7 -> 2; matrix products, arithmetic and copies ran while one was open for 8% -> 37% of each run, Pallas kernels for 0% -> 0%
where the time goes in v1:
time: 1180 us; the launch traced here: 1170 us
  other arithmetic  379 us (32%)
  local copies, waits for them, and re-layouts  281 us (24%)
  waiting for transfers between devices  242 us (21%)
  matrix products  138 us (12%)
  blocking collectives  100 us (8%)
  between operations  19.1 us (2%)
    another operation x31, other arithmetic, local(): low = jnp.tril(jnp.linalg.cholesky(d_full))  168 us
    psum x1, waiting for transfers between devices, local(): d_full = lax.psum(d_part, ('prow', 'pcol'))  148 us
    all_to_all x1, blocking collectives, local(): lax.all_to_all(moved, 'prow', split_axis=0, concat_axis=0, tiled=True)  100 us
    all_to_all x1, waiting for transfers between devices, local(): lax.all_to_all(lax.all_to_all(moved, 'prow', split_axis=0, concat_axis=0,...  94 us
    another operation x3, other arithmetic, local(): jax.scipy.linalg.solve_triangular(low, jnp.eye(panel, dtype=jnp.float32),...  85.5 us
    scatter x2, local copies, waits for them, and re-layouts, route_tables(): recv_pick = jnp.full((parent_len,), groups * capacity, jnp.int32).at[land...  61.1 us
    another operation x5, other arithmetic  37.7 us
    dot_general x1, matrix products, local(): matrix = matrix - jnp.dot(rows_u, cols_u.T, precision=HIGHEST)  33.9 us
  transfers between devices with their start and end apart: 4, of which 2 were waited for; matrix products, arithmetic and copies ran while one was open for 37% of the time, Pallas kernels for 0%

profile of v1, /device:TPU:1, one launch (start us, length us, event | category | flops | bytes accessed | tf_op | source)
XLA Modules:
  0.0 1165.9 jit_solution(9790568696596988251)
XLA Ops:
  7.7 18.0 %reduce-window.16 = s32[8,8,8,128]{3,2,1,0:T(8,128)S(1)} reduce-window(s32[8,8,8,128]{3,2,1,0:T(8,128)S(1)} %fusion.70, s32[]{:T(128)} %copy.223), window={size=1x1x1x128 pad=0_0x0_0x0_0x127_0}, to_apply=%region_4.5 | reduce-window | flops 8323072 | bytes 524292 | tf_op jit(solution)/shard_map/reduce-window.2
  33.1 30.4 %scatter_custom_fusion.1 = s32[2048]{0:T(1024)S(1)} fusion(s32[8192]{0:T(1024)S(1)} %bitcast.183, s32[8192]{0:T(1024)S(1)} %bitcast.182, s32[]{:T(128)} %constant.454.clone.1), kind=kCustom, calls=%fused_computation.246 | custom fusion | bytes 8196 | tf_op jit(solution)/shard_map/scatter | solution.py:53
  83.3 18.1 %reduce-window.14 = s32[16,16,4,128]{3,1,2,0:T(8,128)S(1)} reduce-window(s32[16,16,4,128]{3,1,2,0:T(8,128)S(1)} %fusion.53, s32[]{:T(128)} %copy.223), window={size=1x1x1x128 pad=0_0x0_0x0_0x127_0}, to_apply=%region_0.1 | reduce-window | flops 16646144 | bytes 1048580 | tf_op jit(solution)/shard_map/reduce-window
  105.1 30.6 %scatter_custom_fusion = s32[1024]{0:T(1024)S(1)} fusion(s32[8192]{0:T(1024)S(1)} %get-tuple-element.96, s32[8192]{0:T(1024)S(1)} %bitcast.184, s32[]{:T(128)} %constant.444.clone.1), kind=kCustom, calls=%fused_computation.255 | custom fusion | bytes 4100 | tf_op jit(solution)/shard_map/scatter | solution.py:53
  164.1 100.2 %all_to_all.10 = f32[8,256,16,64]{1,3,2,0:T(8,128)S(1)} all-to-all(f32[8,256,16,64]{1,3,2,0:T(8,128)S(1)} %copy_select_fusion), channel_id=1, replica_groups=mesh['prow'=8,'pcol'=16] {'prow'}, dimensions={0} | all-to-all | bytes 16777216 | tf_op jit(solution)/shard_map/all_to_all | solution.py:126
  275.1 29.6 %reduce.48 = f32[4,512,2,512]{3,2,1,0:T(2,128)} reduce(f32[4,1,512,2,1,512]{5,4,3,2,1,0:T(1,128)} %param.3, f32[]{:T(128)} %constant.492), dimensions={1,4}, to_apply=%param.3.reduce_sub_computation | reduce | bytes 16777220 | tf_op args[0]
  322.5 94.0 %all-to-all-done.1 = f32[8,256,16,64]{1,3,0,2:T(8,128)} async-done(((f32[8,256,16,64]{1,3,0,2:T(8,128)}), f32[8,256,16,64]{1,3,0,2:T(8,128)}, u32[]{:S(2)}, u32[]{:S(2)}) %all-to-all-start.1) | async-done | bytes 8388640 | tf_op jit(solution)/shard_map/all_to_all | solution.py:125
  416.5 14.5 %copy.159 = f32[8,256,16,64]{3,2,1,0:T(8,128)} copy(f32[8,256,16,64]{1,3,0,2:T(8,128)} %all-to-all-done.1) | data formatting | bytes 16777216 | tf_op jit(solution)/shard_map/reshape | solution.py:132
  431.1 14.5 %reshape.396 = f32[2048,1024]{1,0:T(8,128)} reshape(f32[8,256,16,64]{3,2,1,0:T(8,128)} %copy.159) | data formatting | bytes 16777216 | tf_op jit(solution)/shard_map/reshape | solution.py:132
  453.6 16.1 %gather_fusion.2 = f32[2048,1025]{1,0:T(8,128)} fusion(f32[2049,1025]{1,0:T(8,128)} %pad.10, s32[2048]{0:T(1024)S(1)} %get-tuple-element.106), kind=kCustom, calls=%fused_computation.2 | custom fusion | bytes 16801792 | tf_op jit(solution)/shard_map/jit(_take)/gather | solution.py:133
  487.1 12.4 %gather_fusion.3 = f32[1024,2048]{1,0:T(8,128)} fusion(f32[2048,1025]{0,1:T(8,128)} %copy.128, s32[1024]{0:T(1024)S(1)} %get-tuple-element.108), kind=kCustom, calls=%fused_computation.3 | custom fusion | bytes 16781312 | tf_op jit(solution)/shard_map/jit(_take)/gather | solution.py:133
  527.3 147.5 %all-reduce.7.cloned.1.call-done = f32[1024,1024]{0,1:T(8,128)} async-done(((f32[1024,1024]{0,1:T(8,128)}), f32[1024,1024]{0,1:T(8,128)}) %all-reduce.7.cloned.1.call-update) | async-done | bytes 4194320 | tf_op jit(solution)/shard_map/psum | solution.py:165
  686.7 11.7 %cholesky.223 = f32[128,128]{1,0:T(8,128)S(1)} custom-call(f32[128,128]{1,0:T(8,128)S(1)} %cholesky.580), custom_call_target="Cholesky" | custom-call | tf_op jit(solution)/shard_map/jit(cholesky)/cholesky | solution.py:166
  711.4 11.7 %cholesky.244 = f32[128,128]{1,0:T(8,128)S(1)} custom-call(f32[128,128]{1,0:T(8,128)S(1)} %cholesky.584), custom_call_target="Cholesky" | custom-call | tf_op jit(solution)/shard_map/jit(cholesky)/cholesky | solution.py:166
  741.5 11.7 %cholesky.468 = f32[128,128]{1,0:T(8,128)S(1)} custom-call(f32[128,128]{1,0:T(8,128)S(1)} %cholesky.589), custom_call_target="Cholesky" | custom-call | tf_op jit(solution)/shard_map/jit(cholesky)/cholesky | solution.py:166
  768.7 11.7 %cholesky.487 = f32[128,128]{1,0:T(8,128)S(1)} custom-call(f32[128,128]{1,0:T(8,128)S(1)} %cholesky.594), custom_call_target="Cholesky" | custom-call | tf_op jit(solution)/shard_map/jit(cholesky)/cholesky | solution.py:166
  795.3 11.9 %cholesky.506 = f32[128,128]{1,0:T(8,128)S(1)} custom-call(f32[128,128]{1,0:T(8,128)S(1)} %cholesky.599), custom_call_target="Cholesky" | custom-call | tf_op jit(solution)/shard_map/jit(cholesky)/cholesky | solution.py:166
  822.0 11.7 %cholesky.526 = f32[128,128]{1,0:T(8,128)S(1)} custom-call(f32[128,128]{1,0:T(8,128)S(1)} %cholesky.604), custom_call_target="Cholesky" | custom-call | tf_op jit(solution)/shard_map/jit(cholesky)/cholesky | solution.py:166
  903.4 23.3 %while.1 = (s32[]{:T(128)}, f32[1024,1024]{0,1:T(8,128)}, s32[8,2]{0,1:T(2,128)S(1)}, f32[8,128,128]{2,1,0:T(8,128)S(1)}, s32[]{:T(128)}) while((s32[]{:T(128)}, f32[1024,1024]{0,1:T(8,128)}, s32[8,2]{0,1:T(2,128)S(1)}, f32[8,128,128]{2,1,0:T(8,128)S(1)}, s32[]{:T(128)}) %tuple.67), condition=%wide.while_cond, body=%wide.while_body.sunk | while | flops 2 | bytes 393321 | solution.py:167
  926.7 78.8 %custom-call.70 = f32[8,128,128]{1,2,0:T(8,128)S(1)} custom-call(f32[8,128,128]{2,1,0:T(8,128)S(1)} %get-tuple-element.12), custom_call_target="InvertDiagBlocksLowerTriangular" | custom-call | tf_op jit(solution)/shard_map/jit(_solve_triangular)/triangular_solve | solution.py:167
  1034.1 17.7 %fusion.125 = f32[1024,1024]{0,1:T(8,128)} fusion(f32[1024,1024]{0,1:T(8,128)} %all-reduce.11.cloned.1.call-done, f32[1024,1024]{1,0:T(8,128)} %convolution_dynamic-update-slice_fusion), kind=kOutput, calls=%fused_computation.287 | convolution fusion | flops 12884901888 | bytes 12582912 | tf_op jit(solution)/shard_map/dot_general | solution.py:171
  1051.8 30.2 %fusion.124 = f32[2048,1024]{0,1:T(8,128)S(1)} fusion(f32[2048,1024]{0,1:T(8,128)} %all-reduce.9.cloned.1.call-done, f32[1024,1024]{1,0:T(8,128)} %convolution_dynamic-update-slice_fusion), kind=kOutput, calls=%fused_computation.286 | convolution fusion | flops 25769803776 | bytes 20971520 | tf_op jit(solution)/shard_map/dot_general | solution.py:170
  1085.7 33.9 %fusion.15 = f32[2048,1024]{0,1:T(8,128)} fusion(f32[2048,1024]{0,1:T(8,128)} %copy-done, f32[1024,1024]{0,1:T(8,128)S(1)} %copy-done.5, f32[1536,1024]{0,1:T(8,128)S(1)} %slice.325, f32[512,1024]{0,1:T(8,128)S(1)} %slice_select_fusion.2, s32[2048]{0:T(1024)S(1)} %bitcast.185, pred[2048]{0:T(1024)(128)(4,1)S(1)} %bitcast.187, pred[1024]{0:T(1024)(128)(4,1)S(1)} %ge.77), kind=kOutput, calls=%fused_computation.42 | convolution fusion | flops 25781338112 | bytes 29371392 | tf_op jit(solution)/shard_map/dot_general | solution.py:181
  1138.7 20.5 %copy.149 = f32[4,1,512,2,1,512]{5,4,3,2,1,0:T(1,128)} copy(f32[4,1,512,2,1,512]{2,0,5,3,4,1:T(4,128)} %reshape.302) | data formatting | bytes 16777216 | tf_op jit(solution)/shard_map/reshape | solution.py:188
  (225 shorter events, 368.9 us)
Async XLA Ops:
  6.5 57.1 %copy-start.4 = (f32[2,1,512,1,1,512]{5,4,3,2,1,0:T(1,128)S(1)}, f32[2,1,512,1,1,512]{5,4,3,2,1,0:T(1,128)}, u32[]{:S(2)}) copy-start(f32[2,1,512,1,1,512]{5,4,3,2,1,0:T(1,128)} %param.4) | copy-start | bytes 6291460
  268.2 148.4 %all-to-all-start.1 = ((f32[8,256,16,64]{1,3,0,2:T(8,128)}), f32[8,256,16,64]{1,3,0,2:T(8,128)}, u32[]{:S(2)}, u32[]{:S(2)}) async-start(f32[8,256,16,64]{1,3,0,2:T(8,128)} %copy.125), calls=%async_computation.1 | async-start | bytes 16777216 | tf_op jit(solution)/shard_map/all_to_all | solution.py:125
  275.0 399.8 %all-reduce.7.cloned.1.call-start = ((), (), s32[]{:S(2)}) async-start(), calls=%async_computation.2 | async-start | bytes 8388608 | tf_op jit(solution)/shard_map/psum | solution.py:165
  506.0 3.4 copy-start
  512.5 521.6 %all-reduce.11.cloned.1.call-start = ((), (), s32[]{:S(2)}) async-start(), calls=%async_computation.4 | async-start | bytes 8388608 | tf_op jit(solution)/shard_map/psum | solution.py:164
  517.1 534.7 %all-reduce.9.cloned.1.call-start = ((), (), s32[]{:S(2)}) async-start(), calls=%async_computation.3 | async-start | bytes 16777216 | tf_op jit(solution)/shard_map/psum | solution.py:163
  684.8 1.9 copy-start.2
  1005.5 4.7 copy-start.1
  1082.0 2.2 copy-start.3
  1082.7 3.0 copy-start.5
Sparse Core Ops, SparseCore 0:
  512.6 162.1 all-reduce.6
  677.1 69.6 all-reduce.10
  750.4 142.7 all-reduce.8

commit v2 on v1

--- a/solution.py
+++ b/solution.py
@@ -118,16 +118,14 @@
     col_send, col_recv = route_tables(
         child_to_parent, child_cblocks, grid_cols, block_width, my_col, cap_cols, local_cols
     )
-    padded = jnp.pad(child_block.reshape(child_rows, child_cols), ((0, 1), (0, 1)))
-    moved = jnp.take(jnp.take(padded, row_send, axis=0), col_send, axis=1).reshape(
-        grid_rows, cap_rows, grid_cols, cap_cols
-    )
+    child_local = child_block.reshape(child_rows, child_cols)
+    staged = jnp.take(jnp.pad(child_local, ((0, 0), (0, 1))), col_send, axis=1)
+    staged = lax.all_to_all(
+        staged.reshape(child_rows, grid_cols, cap_cols), "pcol", split_axis=1, concat_axis=1, tiled=True
+    ).reshape(child_rows, grid_cols * cap_cols)
+    moved = jnp.take(jnp.pad(staged, ((0, 1), (0, 0))), row_send, axis=0)
     moved = lax.all_to_all(
-        lax.all_to_all(moved, "prow", split_axis=0, concat_axis=0, tiled=True),
-        "pcol",
-        split_axis=2,
-        concat_axis=2,
-        tiled=True,
+        moved.reshape(grid_rows, cap_rows, grid_cols * cap_cols), "prow", split_axis=0, concat_axis=0, tiled=True
     )
     arrived = jnp.pad(moved.reshape(grid_rows * cap_rows, grid_cols * cap_cols), ((0, 1), (0, 1)))
     added = jnp.take(jnp.take(arrived, row_recv, axis=0), col_recv, axis=1)
@@ -145,9 +143,23 @@
     y_part = jnp.concatenate(
         [jnp.where(my_row == p, first_rows, zero_rows) for p in range(NP)], axis=0
     )
-    corner = first_rows[:, :block_width]
+    panel_ids = jnp.arange(panel, dtype=jnp.int32)
+    child_row_ids = (
+        (jnp.arange(child_rblocks, dtype=jnp.int32)[:, None] * grid_rows + my_row) * block_width
+        + jnp.arange(block_width, dtype=jnp.int32)[None, :]
+    ).reshape(-1)
+    child_col_ids = (
+        (jnp.arange(child_cblocks, dtype=jnp.int32)[:, None] * grid_cols + my_col) * block_width
+        + jnp.arange(block_width, dtype=jnp.int32)[None, :]
+    ).reshape(-1)
+    row_hit = (child_to_parent[child_row_ids][None, :] == panel_ids[:, None]).astype(jnp.float32)
+    col_hit = (child_to_parent[child_col_ids][None, :] == panel_ids[:, None]).astype(jnp.float32)
+    corner_child = jnp.dot(
+        jnp.dot(row_hit, child_local, precision=HIGHEST), col_hit.T, precision=HIGHEST
+    )
+    corner = front.reshape(local_rows, local_cols)[:block_width, :block_width]
     zero_corner = jnp.zeros_like(corner)
-    d_part = jnp.concatenate(
+    d_part = corner_child + jnp.concatenate(
         [
             jnp.concatenate(
                 [

time: 1180 us -> 983 us (0.83)
  blocking collectives: 100 us -> 0 us
  waiting for transfers between devices: 242 us -> 142 us
  local copies, waits for them, and re-layouts: 281 us -> 266 us
  starting transfers between devices: 6.93 us -> 19.1 us
    all_to_all x1 -> x0, blocking collectives: 100 us -> none  [local(): lax.all_to_all(moved, 'prow', split_axis=0, concat_axis=0, tiled=True)]
    all_to_all x1 -> x2, waiting for transfers between devices: 94 us -> 3.49 us  [the longest x1 3.49 us: local(): lax.all_to_all(staged.reshape(child_rows, grid_cols, cap_cols), 'pcol', s...]
    psum x1, waiting for transfers between devices: 148 us -> 83.6 us  [local(): d_full = lax.psum(d_part, ('prow', 'pcol'))]
    psum x1, waiting for transfers between devices: 0.01 us -> 55.1 us  [local(): x_full = lax.psum(x_part, 'pcol')]
    reshape x3, local copies, waits for them, and re-layouts: 38.1 us -> 16.3 us  [the longest x1 9.13 us: local(): corner = front.reshape(local_rows, local_cols)[:block_width, :block_width]]
    all_to_all x1 -> x2, starting transfers between devices: 6.81 us -> 19 us  [the longest x1 11.4 us: local(): lax.all_to_all(moved.reshape(grid_rows, cap_rows, grid_cols * cap_cols),...]
    gather x2 -> x4, local copies, waits for them, and re-layouts: 20.4 us -> 28.6 us  [the longest x1 13.9 us: local(): moved = jnp.take(jnp.pad(staged, ((0, 1), (0, 0))), row_send, axis=0)]
    unnamed x21 -> x27, local copies, waits for them, and re-layouts: 27.5 us -> 19.6 us
  transfers between devices with their start and end apart: 4 -> 5, of which waited for: 2 -> 3; matrix products, arithmetic and copies ran while one was open for 37% -> 51% of each run, Pallas kernels for 0% -> 0%
where the time goes in v2:
time: 983 us; the launch traced here: 971 us
  other arithmetic  374 us (38%)
  local copies, waits for them, and re-layouts  266 us (27%)
  matrix products  148 us (15%)
  waiting for transfers between devices  142 us (14%)
  between operations  20.8 us (2%)
  starting transfers between devices  19.1 us (2%)
    another operation x31, other arithmetic, local(): low = jnp.tril(jnp.linalg.cholesky(d_full))  168 us
    another operation x3, other arithmetic, local(): jax.scipy.linalg.solve_triangular(low, jnp.eye(panel, dtype=jnp.float32),...  85.4 us
    psum x1, waiting for transfers between devices, local(): d_full = lax.psum(d_part, ('prow', 'pcol'))  83.6 us
    scatter x2, local copies, waits for them, and re-layouts, route_tables(): recv_pick = jnp.full((parent_len,), groups * capacity, jnp.int32).at[land...  61.1 us
    psum x1, waiting for transfers between devices, local(): x_full = lax.psum(x_part, 'pcol')  55.1 us
    another operation x5, other arithmetic  37.7 us
    dot_general x1, matrix products, local(): matrix = matrix - jnp.dot(rows_u, cols_u.T, precision=HIGHEST)  34 us
    reshape x2, local copies, waits for them, and re-layouts, local(): return matrix.reshape(front.shape)  31.3 us
  transfers between devices with their start and end apart: 5, of which 3 were waited for; matrix products, arithmetic and copies ran while one was open for 51% of the time, Pallas kernels for 0%

profile of v2, /device:TPU:1, one launch (start us, length us, event | category | flops | bytes accessed | tf_op | source)
XLA Modules:
  0.0 971.2 jit_solution(18167670625170066915)
XLA Ops:
  7.4 29.2 %reduce.48 = f32[4,512,2,512]{3,2,1,0:T(2,128)} reduce(f32[4,1,512,2,1,512]{5,4,3,2,1,0:T(1,128)} %param.3, f32[]{:T(128)} %constant.501), dimensions={1,4}, to_apply=%param.3.reduce_sub_computation | reduce | bytes 16777220 | tf_op args[0]
  54.6 18.1 %reduce-window.14 = s32[16,16,4,128]{3,1,2,0:T(8,128)S(1)} reduce-window(s32[16,16,4,128]{3,1,2,0:T(8,128)S(1)} %fusion.56, s32[]{:T(128)} %copy.160), window={size=1x1x1x128 pad=0_0x0_0x0_0x127_0}, to_apply=%region_17.18 | reduce-window | flops 16646144 | bytes 1048580 | tf_op jit(solution)/shard_map/reduce-window
  77.1 30.7 %scatter_custom_fusion = s32[1024]{0:T(1024)S(1)} fusion(s32[8192]{0:T(1024)S(1)} %get-tuple-element.88, s32[8192]{0:T(1024)S(1)} %bitcast.192, s32[]{:T(128)} %constant.463.clone.1), kind=kCustom, calls=%fused_computation.267 | custom fusion | bytes 4100 | tf_op jit(solution)/shard_map/scatter | solution.py:53
  152.0 18.0 %reduce-window.16 = s32[8,8,8,128]{3,2,1,0:T(8,128)S(1)} reduce-window(s32[8,8,8,128]{3,2,1,0:T(8,128)S(1)} %fusion.73, s32[]{:T(128)} %copy.160), window={size=1x1x1x128 pad=0_0x0_0x0_0x127_0}, to_apply=%region_21.22 | reduce-window | flops 8323072 | bytes 524292 | tf_op jit(solution)/shard_map/reduce-window.2
  179.5 30.4 %scatter_custom_fusion.1 = s32[2048]{0:T(1024)S(1)} fusion(s32[8192]{0:T(1024)S(1)} %bitcast.190, s32[8192]{0:T(1024)S(1)} %bitcast.191, s32[]{:T(128)} %constant.472.clone.1), kind=kCustom, calls=%fused_computation.256 | custom fusion | bytes 8196 | tf_op jit(solution)/shard_map/scatter | solution.py:53
  223.8 13.9 %gather_fusion.3 = f32[2048,1024]{1,0:T(8,128)} fusion(f32[1025,1024]{1,0:T(8,128)} %pad.14, s32[2048]{0:T(1024)S(1)} %fusion.108), kind=kCustom, calls=%fused_computation.3 | custom fusion | bytes 16785408 | tf_op jit(solution)/shard_map/jit(_take)/gather | solution.py:126
  257.5 83.6 %all-reduce.8.cloned.1.call-done = f32[1024,1024]{0,1:T(8,128)} async-done(((f32[1024,1024]{0,1:T(8,128)}), f32[1024,1024]{0,1:T(8,128)}) %all-reduce.8.cloned.1.call-update) | async-done | bytes 4194320 | tf_op jit(solution)/shard_map/psum | solution.py:177
  341.1 13.8 %copy.60 = f32[1024,1024]{1,0:T(8,128)} copy(f32[1024,1024]{0,1:T(8,128)} %all-reduce.8.cloned.1.call-done) | data formatting | bytes 8388608 | tf_op jit(solution)/shard_map/psum | solution.py:177
  361.3 11.7 %cholesky.224 = f32[128,128]{1,0:T(8,128)S(1)} custom-call(f32[128,128]{1,0:T(8,128)S(1)} %cholesky.583), custom_call_target="Cholesky" | custom-call | tf_op jit(solution)/shard_map/jit(cholesky)/cholesky | solution.py:178
  386.3 11.7 %cholesky.245 = f32[128,128]{1,0:T(8,128)S(1)} custom-call(f32[128,128]{1,0:T(8,128)S(1)} %cholesky.587), custom_call_target="Cholesky" | custom-call | tf_op jit(solution)/shard_map/jit(cholesky)/cholesky | solution.py:178
  416.1 11.7 %cholesky.470 = f32[128,128]{1,0:T(8,128)S(1)} custom-call(f32[128,128]{1,0:T(8,128)S(1)} %cholesky.592), custom_call_target="Cholesky" | custom-call | tf_op jit(solution)/shard_map/jit(cholesky)/cholesky | solution.py:178
  443.2 11.7 %cholesky.489 = f32[128,128]{1,0:T(8,128)S(1)} custom-call(f32[128,128]{1,0:T(8,128)S(1)} %cholesky.597), custom_call_target="Cholesky" | custom-call | tf_op jit(solution)/shard_map/jit(cholesky)/cholesky | solution.py:178
  469.8 11.8 %cholesky.508 = f32[128,128]{1,0:T(8,128)S(1)} custom-call(f32[128,128]{1,0:T(8,128)S(1)} %cholesky.602), custom_call_target="Cholesky" | custom-call | tf_op jit(solution)/shard_map/jit(cholesky)/cholesky | solution.py:178
  496.5 11.7 %cholesky.528 = f32[128,128]{1,0:T(8,128)S(1)} custom-call(f32[128,128]{1,0:T(8,128)S(1)} %cholesky.607), custom_call_target="Cholesky" | custom-call | tf_op jit(solution)/shard_map/jit(cholesky)/cholesky | solution.py:178
  522.7 11.7 %cholesky.548 = f32[128,128]{1,0:T(8,128)S(1)} custom-call(f32[128,128]{1,0:T(8,128)S(1)} %cholesky.612), custom_call_target="Cholesky" | custom-call | tf_op jit(solution)/shard_map/jit(cholesky)/cholesky | solution.py:178
  559.9 16.0 %gather_fusion.4 = f32[2048,1025]{1,0:T(8,128)} fusion(f32[2049,1025]{1,0:T(8,128)} %pad.15, s32[2048]{0:T(1024)S(1)} %fusion.107), kind=kCustom, calls=%fused_computation.4 | custom fusion | bytes 16801792 | tf_op jit(solution)/shard_map/jit(_take)/gather | solution.py:131
  593.4 12.4 %gather_fusion.5 = f32[1024,2048]{1,0:T(8,128)} fusion(f32[2048,1025]{0,1:T(8,128)} %copy.82, s32[1024]{0:T(1024)S(1)} %get-tuple-element.100), kind=kCustom, calls=%fused_computation.5 | custom fusion | bytes 16781312 | tf_op jit(solution)/shard_map/jit(_take)/gather | solution.py:131
  651.6 24.2 %while.1 = (s32[]{:T(128)}, f32[1024,1024]{0,1:T(8,128)}, s32[8,2]{0,1:T(2,128)S(1)}, f32[8,128,128]{2,1,0:T(8,128)S(1)}, s32[]{:T(128)}) while((s32[]{:T(128)}, f32[1024,1024]{0,1:T(8,128)}, s32[8,2]{0,1:T(2,128)S(1)}, f32[8,128,128]{2,1,0:T(8,128)S(1)}, s32[]{:T(128)}) %tuple.65), condition=%wide.while_cond, body=%wide.while_body.sunk | while | flops 2 | bytes 393321 | solution.py:179
  675.7 78.8 %custom-call.70 = f32[8,128,128]{1,2,0:T(8,128)S(1)} custom-call(f32[8,128,128]{2,1,0:T(8,128)S(1)} %get-tuple-element.12), custom_call_target="InvertDiagBlocksLowerTriangular" | custom-call | tf_op jit(solution)/shard_map/jit(_solve_triangular)/triangular_solve | solution.py:179
  783.2 17.7 %fusion.128 = f32[1024,1024]{0,1:T(8,128)} fusion(f32[1024,1024]{0,1:T(8,128)} %all-reduce.12.cloned.1.call-done, f32[1024,1024]{1,0:T(8,128)} %convolution_dynamic-update-slice_fusion), kind=kOutput, calls=%fused_computation.300 | convolution fusion | flops 12884901888 | bytes 12582912 | tf_op jit(solution)/shard_map/dot_general | solution.py:183
  801.0 55.1 %all-reduce.10.cloned.1.call-done = f32[2048,1024]{0,1:T(8,128)} async-done(((f32[2048,1024]{0,1:T(8,128)}), f32[2048,1024]{0,1:T(8,128)}) %all-reduce.10.cloned.1.call-update) | async-done | bytes 8388624 | tf_op jit(solution)/shard_map/psum | solution.py:175
  856.1 30.2 %fusion.127 = f32[2048,1024]{0,1:T(8,128)S(1)} fusion(f32[2048,1024]{0,1:T(8,128)} %all-reduce.10.cloned.1.call-done, f32[1024,1024]{1,0:T(8,128)} %convolution_dynamic-update-slice_fusion), kind=kOutput, calls=%fused_computation.299 | convolution fusion | flops 25769803776 | bytes 20971520 | tf_op jit(solution)/shard_map/dot_general | solution.py:182
  890.0 34.0 %fusion.16 = f32[2048,1024]{0,1:T(8,128)} fusion(f32[2048,1024]{0,1:T(8,128)} %copy-done.1, f32[1024,1024]{0,1:T(8,128)S(1)} %copy-done.8, f32[1536,1024]{0,1:T(8,128)S(1)} %slice.328, f32[512,1024]{0,1:T(8,128)S(1)} %slice_select_fusion.2, s32[2048]{0:T(1024)S(1)} %bitcast.195, pred[2048]{0:T(1024)(128)(4,1)S(1)} %bitcast.198, ...), kind=kOutput, calls=%fused_computation.46 | convolution fusion | flops 25781338112 | bytes 29371392 | tf_op jit(solution)/shard_map/dot_general | solution.py:193
  943.0 20.5 %copy.87 = f32[4,1,512,2,1,512]{5,4,3,2,1,0:T(1,128)} copy(f32[4,1,512,2,1,512]{2,0,5,3,4,1:T(4,128)} %reshape.380) | data formatting | bytes 16777216 | tf_op jit(solution)/shard_map/reshape | solution.py:200
  (241 shorter events, 365.4 us)
Async XLA Ops:
  7.4 333.7 %all-reduce.8.cloned.1.call-start = ((), (), s32[]{:S(2)}) async-start(), calls=%async_computation.2 | async-start | bytes 8388608 | tf_op jit(solution)/shard_map/psum | solution.py:177
  45.3 9.1 copy-start
  144.3 69.5 %all-to-all-start = ((f32[1024,16,64]{0,2,1:T(8,128)}), f32[1024,16,64]{0,2,1:T(8,128)}, u32[]{:S(2)}, u32[]{:S(2)}) async-start(f32[1024,16,64]{0,2,1:T(8,128)} %broadcast_select_fusion.2), calls=%async_computation | async-start | bytes 8388608 | tf_op jit(solution)/shard_map/all_to_all | solution.py:123
  243.6 308.3 %all-to-all-start.1 = ((f32[8,256,1024]{2,1,0:T(8,128)}), f32[8,256,1024]{2,1,0:T(8,128)}, u32[]{:S(2)}, u32[]{:S(2)}) async-start(f32[8,256,1024]{2,1,0:T(8,128)} %broadcast_select_fusion.1), calls=%async_computation.1 | async-start | bytes 16777216 | tf_op jit(solution)/shard_map/all_to_all | solution.py:127
  255.0 528.2 %all-reduce.12.cloned.1.call-start = ((), (), s32[]{:S(2)}) async-start(), calls=%async_computation.4 | async-start | bytes 8388608 | tf_op jit(solution)/shard_map/psum | solution.py:176
  359.4 1.9 copy-start.3
  612.7 3.4 copy-start.1
  619.0 237.0 %all-reduce.10.cloned.1.call-start = ((), (), s32[]{:S(2)}) async-start(), calls=%async_computation.3 | async-start | bytes 16777216 | tf_op jit(solution)/shard_map/psum | solution.py:175
  754.5 4.8 copy-start.2
  886.3 2.2 copy-start.4
  887.0 2.0 copy-start.5
  887.0 2.0 copy-start.6
  887.0 2.0 copy-start.7
  887.0 3.0 copy-start.8
Sparse Core Ops, SparseCore 0:
  128.3 212.7 all-reduce.7
Sparse Core Ops, SparseCore 1:
  619.1 91.6 all-reduce.11
  714.3 141.7 all-reduce.9

commit v3 on v2

--- a/solution.py
+++ b/solution.py
@@ -4,6 +4,7 @@
 from jax.sharding import PartitionSpec as P
 
 NP = 2
+SB = 32
 
 
 HIGHEST = lax.Precision.HIGHEST
@@ -29,28 +30,36 @@
 
 def route_tables(mapping, blocks_local, groups, block_width, my_index, capacity, parent_len):
     local_len = blocks_local * block_width
-    parent_blk = mapping // block_width
-    dest_group = by_source(parent_blk % groups, blocks_local, groups, block_width)
-    parent_pos = by_source(
-        parent_blk // groups * block_width + mapping % block_width,
-        blocks_local,
-        groups,
-        block_width,
-    )
-    slot_rank = slot_ranks(dest_group, groups)
-    own_dest = lax.dynamic_index_in_dim(dest_group, my_index, 0, keepdims=False)
-    own_slot = lax.dynamic_index_in_dim(slot_rank, my_index, 0, keepdims=False)
-    send_pick = (
-        jnp.full((groups * capacity,), local_len, jnp.int32)
-        .at[own_dest * capacity + own_slot]
-        .set(jnp.arange(local_len, dtype=jnp.int32))
-    )
-    flat_slot = jnp.arange(groups, dtype=jnp.int32)[:, None] * capacity + slot_rank
-    landing = jnp.where(dest_group == my_index, parent_pos, parent_len)
-    recv_pick = (
-        jnp.full((parent_len,), groups * capacity, jnp.int32)
-        .at[landing.reshape(-1)]
-        .set(flat_slot.reshape(-1), mode="drop")
+    num_groups = local_len // SB
+    group_slots = capacity // SB
+    src_map = by_source(mapping, blocks_local, groups, block_width)
+    dest_g = (src_map[:, ::SB] // block_width) % groups
+    rank_g = slot_ranks(dest_g, groups)
+    group_ids = jnp.arange(num_groups, dtype=jnp.int32)
+    lane = jnp.arange(SB, dtype=jnp.int32)
+    own_dest = lax.dynamic_index_in_dim(dest_g, my_index, 0, keepdims=False)
+    own_rank = lax.dynamic_index_in_dim(rank_g, my_index, 0, keepdims=False)
+    slot_ids = jnp.arange(groups * group_slots, dtype=jnp.int32)
+    hit = (own_dest[None, :] == (slot_ids // group_slots)[:, None]) & (
+        own_rank[None, :] == (slot_ids % group_slots)[:, None]
+    )
+    picked = jnp.sum(jnp.where(hit, group_ids[None, :], 0), axis=1)
+    send_pick = jnp.where(
+        jnp.any(hit, axis=1)[:, None], picked[:, None] * SB + lane[None, :], local_len
+    ).reshape(-1)
+    hit_in = (dest_g[:, None, :] == my_index) & (
+        rank_g[:, None, :] == jnp.arange(group_slots, dtype=jnp.int32)[None, :, None]
+    )
+    picked_in = jnp.sum(jnp.where(hit_in, group_ids[None, None, :], 0), axis=2)
+    elem = (picked_in[:, :, None] * SB + lane[None, None, :]).reshape(groups, capacity)
+    parent_of_slot = jnp.take_along_axis(src_map, elem, axis=1)
+    parent_blk = parent_of_slot // block_width
+    landing = parent_blk // groups * block_width + parent_of_slot % block_width
+    valid = jnp.repeat(jnp.any(hit_in, axis=2), SB, axis=1)
+    landing = jnp.where(valid, landing, parent_len).reshape(-1)
+    match = landing[None, :] == jnp.arange(parent_len, dtype=jnp.int32)[:, None]
+    recv_pick = jnp.where(
+        jnp.any(match, axis=1), jnp.argmax(match, axis=1).astype(jnp.int32), groups * capacity
     )
     return (send_pick, recv_pick)
 

time: 983 us -> 935 us (0.951)
  local copies, waits for them, and re-layouts: 266 us -> 213 us
  waiting for transfers between devices: 142 us -> 168 us
  other arithmetic: 374 us -> 352 us
    scatter x4 -> x0, local copies, waits for them, and re-layouts: 67.9 us -> none  [the longest x2 61.1 us: route_tables(): recv_pick = jnp.full((parent_len,), groups * capacity, jnp.int32).at[land...]
    all_to_all x1, waiting for transfers between devices: 3.49 us -> 32.5 us  [local(): lax.all_to_all(staged.reshape(child_rows, grid_cols, cap_cols), 'pcol', s...]
    another operation x5 -> x4, other arithmetic: 37.7 us -> 10.9 us  [the longest x2 9.7 us: route_tables(): jnp.argmax(match, axis=1).astype(jnp.int32)]
    gather x0 -> x3, local copies, waits for them, and re-layouts: none -> 21.7 us  [route_tables(): parent_of_slot = jnp.take_along_axis(src_map, elem, axis=1)]
    another operation x46 -> x41, local copies, waits for them, and re-layouts: 25.8 us -> 25.2 us
    unnamed x5 -> x4, other arithmetic: 29.4 us -> 29.6 us
  transfers between devices with their start and end apart: 5 -> 5, of which waited for: 3 -> 3; matrix products, arithmetic and copies ran while one was open for 51% -> 49% of each run, Pallas kernels for 0% -> 0%
where the time goes in v3:
time: 935 us; the launch traced here: 927 us
  other arithmetic  352 us (38%)
  local copies, waits for them, and re-layouts  213 us (23%)
  waiting for transfers between devices  168 us (18%)
  matrix products  148 us (16%)
  starting transfers between devices  24 us (3%)
  between operations  21.2 us (2%)
    another operation x31, other arithmetic, local(): low = jnp.tril(jnp.linalg.cholesky(d_full))  169 us
    another operation x3, other arithmetic, local(): jax.scipy.linalg.solve_triangular(low, jnp.eye(panel, dtype=jnp.float32),...  85.6 us
    psum x1, waiting for transfers between devices, local(): d_full = lax.psum(d_part, ('prow', 'pcol'))  81.2 us
    psum x1, waiting for transfers between devices, local(): x_full = lax.psum(x_part, 'pcol')  54.1 us
    dot_general x1, matrix products, local(): matrix = matrix - jnp.dot(rows_u, cols_u.T, precision=HIGHEST)  34 us
    all_to_all x1, waiting for transfers between devices, local(): lax.all_to_all(staged.reshape(child_rows, grid_cols, cap_cols), 'pcol', s...  32.5 us
    reshape x2, local copies, waits for them, and re-layouts, local(): return matrix.reshape(front.shape)  31.3 us
    dot_general x1, matrix products, local(): rows_f = jnp.dot(x_full, low_inv.T, precision=HIGHEST)  30 us
  transfers between devices with their start and end apart: 5, of which 3 were waited for; matrix products, arithmetic and copies ran while one was open for 49% of the time, Pallas kernels for 0%

profile of v3, /device:TPU:1, one launch (start us, length us, event | category | flops | bytes accessed | tf_op | source)
XLA Modules:
  0.0 926.6 jit_solution(5729829548659577808)
XLA Ops:
  24.5 29.5 %reduce.84 = f32[4,512,2,512]{3,2,1,0:T(2,128)} reduce(f32[4,1,512,2,1,512]{5,4,3,2,1,0:T(1,128)} %param.3, f32[]{:T(128)} %constant.634), dimensions={1,4}, to_apply=%param.3.reduce_sub_computation | reduce | bytes 16777220 | tf_op args[0]
  117.3 13.0 %gather_fusion.7 = s32[2048]{0:T(1024)S(1)} fusion(s32[8,1024]{1,0:T(8,128)S(1)} %bitcast.153, s32[2048]{0:T(1024)S(1)} %bitcast.154), kind=kCustom, calls=%fused_computation.7 | custom fusion | bytes 32768 | tf_op jit(solution)/shard_map/jit(take_along_axis)/gather | solution.py:55
  141.9 32.5 %all-to-all-done = f32[1024,16,64]{0,2,1:T(8,128)} async-done(((f32[1024,16,64]{0,2,1:T(8,128)}), f32[1024,16,64]{0,2,1:T(8,128)}, u32[]{:S(2)}, u32[]{:S(2)}) %all-to-all-start) | async-done | bytes 4194336 | tf_op jit(solution)/shard_map/all_to_all | solution.py:132
  184.6 14.1 %gather_fusion.3 = f32[2048,1024]{1,0:T(8,128)} fusion(f32[1025,1024]{1,0:T(8,128)} %pad.14, s32[2048]{0:T(1024)S(1)} %broadcast_clamp_fusion), kind=kCustom, calls=%fused_computation.3 | custom fusion | bytes 16785408 | tf_op jit(solution)/shard_map/jit(_take)/gather | solution.py:135
  204.4 16.3 %all-to-all-start.1 = ((f32[8,256,1024]{2,1,0:T(8,128)}), f32[8,256,1024]{2,1,0:T(8,128)}, u32[]{:S(2)}, u32[]{:S(2)}) async-start(f32[8,256,1024]{2,1,0:T(8,128)} %broadcast_select_fusion.1), calls=%async_computation.1 | async-start | bytes 16777216 | tf_op jit(solution)/shard_map/all_to_all | solution.py:136
  223.0 81.2 %all-reduce.8.cloned.1.call-done = f32[1024,1024]{0,1:T(8,128)} async-done(((f32[1024,1024]{0,1:T(8,128)}), f32[1024,1024]{0,1:T(8,128)}) %all-reduce.8.cloned.1.call-update) | async-done | bytes 4194320 | tf_op jit(solution)/shard_map/psum | solution.py:186
  316.3 11.7 %cholesky.224 = f32[128,128]{1,0:T(8,128)S(1)} custom-call(f32[128,128]{1,0:T(8,128)S(1)} %cholesky.583), custom_call_target="Cholesky" | custom-call | tf_op jit(solution)/shard_map/jit(cholesky)/cholesky | solution.py:187
  341.3 11.7 %cholesky.245 = f32[128,128]{1,0:T(8,128)S(1)} custom-call(f32[128,128]{1,0:T(8,128)S(1)} %cholesky.587), custom_call_target="Cholesky" | custom-call | tf_op jit(solution)/shard_map/jit(cholesky)/cholesky | solution.py:187
  371.1 11.7 %cholesky.470 = f32[128,128]{1,0:T(8,128)S(1)} custom-call(f32[128,128]{1,0:T(8,128)S(1)} %cholesky.592), custom_call_target="Cholesky" | custom-call | tf_op jit(solution)/shard_map/jit(cholesky)/cholesky | solution.py:187
  398.0 11.7 %cholesky.489 = f32[128,128]{1,0:T(8,128)S(1)} custom-call(f32[128,128]{1,0:T(8,128)S(1)} %cholesky.597), custom_call_target="Cholesky" | custom-call | tf_op jit(solution)/shard_map/jit(cholesky)/cholesky | solution.py:187
  424.6 12.1 %cholesky.508 = f32[128,128]{1,0:T(8,128)S(1)} custom-call(f32[128,128]{1,0:T(8,128)S(1)} %cholesky.602), custom_call_target="Cholesky" | custom-call | tf_op jit(solution)/shard_map/jit(cholesky)/cholesky | solution.py:187
  451.5 11.7 %cholesky.528 = f32[128,128]{1,0:T(8,128)S(1)} custom-call(f32[128,128]{1,0:T(8,128)S(1)} %cholesky.607), custom_call_target="Cholesky" | custom-call | tf_op jit(solution)/shard_map/jit(cholesky)/cholesky | solution.py:187
  477.7 11.7 %cholesky.548 = f32[128,128]{1,0:T(8,128)S(1)} custom-call(f32[128,128]{1,0:T(8,128)S(1)} %cholesky.612), custom_call_target="Cholesky" | custom-call | tf_op jit(solution)/shard_map/jit(cholesky)/cholesky | solution.py:187
  515.2 16.1 %gather_fusion.4 = f32[2048,1025]{1,0:T(8,128)} fusion(f32[2049,1025]{1,0:T(8,128)} %pad.15, s32[2048]{0:T(1024)S(1)} %fusion.120), kind=kCustom, calls=%fused_computation.4 | custom fusion | bytes 16801792 | tf_op jit(solution)/shard_map/jit(_take)/gather | solution.py:140
  548.8 12.4 %gather_fusion.5 = f32[1024,2048]{1,0:T(8,128)} fusion(f32[2048,1025]{0,1:T(8,128)} %copy.114, s32[1024]{0:T(1024)S(1)} %get-tuple-element.109), kind=kCustom, calls=%fused_computation.5 | custom fusion | bytes 16781312 | tf_op jit(solution)/shard_map/jit(_take)/gather | solution.py:140
  575.1 11.7 %cholesky.566 = f32[128,128]{1,0:T(8,128)S(1)} custom-call(f32[128,128]{1,0:T(8,128)S(1)} %convolution_subtract_fusion.11), custom_call_target="Cholesky" | custom-call | tf_op jit(solution)/shard_map/jit(cholesky)/cholesky | solution.py:187
  607.3 24.8 %while.1 = (s32[]{:T(128)}, f32[1024,1024]{0,1:T(8,128)}, s32[8,2]{0,1:T(2,128)S(1)}, f32[8,128,128]{2,1,0:T(8,128)S(1)}, s32[]{:T(128)}) while((s32[]{:T(128)}, f32[1024,1024]{0,1:T(8,128)}, s32[8,2]{0,1:T(2,128)S(1)}, f32[8,128,128]{2,1,0:T(8,128)S(1)}, s32[]{:T(128)}) %tuple.70), condition=%wide.while_cond, body=%wide.while_body.sunk | while | flops 2 | bytes 393321 | solution.py:188
  632.1 79.0 %custom-call.70 = f32[8,128,128]{1,2,0:T(8,128)S(1)} custom-call(f32[8,128,128]{2,1,0:T(8,128)S(1)} %get-tuple-element.16), custom_call_target="InvertDiagBlocksLowerTriangular" | custom-call | tf_op jit(solution)/shard_map/jit(_solve_triangular)/triangular_solve | solution.py:188
  739.7 17.7 %fusion.147 = f32[1024,1024]{0,1:T(8,128)} fusion(f32[1024,1024]{0,1:T(8,128)} %all-reduce.12.cloned.1.call-done, f32[1024,1024]{1,0:T(8,128)} %convolution_dynamic-update-slice_fusion), kind=kOutput, calls=%fused_computation.367 | convolution fusion | flops 12884901888 | bytes 12582912 | tf_op jit(solution)/shard_map/dot_general | solution.py:192
  757.4 54.1 %all-reduce.10.cloned.1.call-done = f32[2048,1024]{0,1:T(8,128)} async-done(((f32[2048,1024]{0,1:T(8,128)}), f32[2048,1024]{0,1:T(8,128)}) %all-reduce.10.cloned.1.call-update) | async-done | bytes 8388624 | tf_op jit(solution)/shard_map/psum | solution.py:184
  811.6 30.0 %fusion.146 = f32[2048,1024]{0,1:T(8,128)S(1)} fusion(f32[2048,1024]{0,1:T(8,128)} %all-reduce.10.cloned.1.call-done, f32[1024,1024]{1,0:T(8,128)} %convolution_dynamic-update-slice_fusion), kind=kOutput, calls=%fused_computation.366 | convolution fusion | flops 25769803776 | bytes 20971520 | tf_op jit(solution)/shard_map/dot_general | solution.py:191
  845.3 34.0 %fusion.18 = f32[2048,1024]{0,1:T(8,128)} fusion(f32[2048,1024]{0,1:T(8,128)} %copy-done.1, f32[1024,1024]{0,1:T(8,128)S(1)} %copy-done.5, f32[1536,1024]{0,1:T(8,128)S(1)} %slice.320, f32[512,1024]{0,1:T(8,128)S(1)} %slice_select_fusion.2, s32[2048]{0:T(1024)S(1)} %bitcast.167, pred[2048]{0:T(1024)(128)(4,1)S(1)} %bitcast.168, pred[1024]{0:T(1024)(128)(4,1)S(1)} %ge.111), kind=kOutput, calls=%fused_computation.50 | convolution fusion | flops 25781338112 | bytes 29371392 | tf_op jit(solution)/shard_map/dot_general | solution.py:202
  887.6 10.8 %reshape.691 = f32[4,1,512,2,1,512]{2,0,5,3,4,1:T(4,128)} reshape(f32[2048,1024]{0,1:T(8,128)} %pad_maximum_fusion.2) | data formatting | bytes 16777216 | tf_op jit(solution)/shard_map/reshape | solution.py:209
  898.4 20.5 %copy.119 = f32[4,1,512,2,1,512]{5,4,3,2,1,0:T(1,128)} copy(f32[4,1,512,2,1,512]{2,0,5,3,4,1:T(4,128)} %reshape.691) | data formatting | bytes 16777216 | tf_op jit(solution)/shard_map/reshape | solution.py:209
  (278 shorter events, 349.7 us)
Async XLA Ops:
  7.4 296.8 %all-reduce.8.cloned.1.call-start = ((), (), s32[]{:S(2)}) async-start(), calls=%async_computation.2 | async-start | bytes 8388608 | tf_op jit(solution)/shard_map/psum | solution.py:186
  9.7 11.7 %copy-start = (s32[8192]{0:T(1024)S(1)}, s32[8192]{0:T(1024)}, u32[]{:S(2)}) copy-start(s32[8192]{0:T(1024)} %param.5) | copy-start | bytes 98308
  107.6 66.8 %all-to-all-start = ((f32[1024,16,64]{0,2,1:T(8,128)}), f32[1024,16,64]{0,2,1:T(8,128)}, u32[]{:S(2)}, u32[]{:S(2)}) async-start(f32[1024,16,64]{0,2,1:T(8,128)} %broadcast_select_fusion.2), calls=%async_computation | async-start | bytes 8388608 | tf_op jit(solution)/shard_map/all_to_all | solution.py:132
  204.4 302.8 %all-to-all-start.1 = ((f32[8,256,1024]{2,1,0:T(8,128)}), f32[8,256,1024]{2,1,0:T(8,128)}, u32[]{:S(2)}, u32[]{:S(2)}) async-start(f32[8,256,1024]{2,1,0:T(8,128)} %broadcast_select_fusion.1), calls=%async_computation.1 | async-start | bytes 16777216 | tf_op jit(solution)/shard_map/all_to_all | solution.py:136
  220.7 519.1 %all-reduce.12.cloned.1.call-start = ((), (), s32[]{:S(2)}) async-start(), calls=%async_computation.4 | async-start | bytes 8388608 | tf_op jit(solution)/shard_map/psum | solution.py:185
  314.4 2.0 copy-start.3
  568.0 3.4 copy-start.1
  574.3 237.2 %all-reduce.10.cloned.1.call-start = ((), (), s32[]{:S(2)}) async-start(), calls=%async_computation.3 | async-start | bytes 16777216 | tf_op jit(solution)/shard_map/psum | solution.py:184
  711.1 4.8 copy-start.2
  841.6 2.2 copy-start.4
  842.3 3.0 copy-start.5
Sparse Core Ops, SparseCore 0:
  92.9 211.2 all-reduce.7
Sparse Core Ops, SparseCore 1:
  574.4 91.7 all-reduce.11
  669.6 141.9 all-reduce.9

commit v4 on v3

--- a/solution.py
+++ b/solution.py
@@ -166,7 +166,7 @@
     corner_child = jnp.dot(
         jnp.dot(row_hit, child_local, precision=HIGHEST), col_hit.T, precision=HIGHEST
     )
-    corner = front.reshape(local_rows, local_cols)[:block_width, :block_width]
+    corner = front[0, 0, :, 0, 0, :]
     zero_corner = jnp.zeros_like(corner)
     d_part = corner_child + jnp.concatenate(
         [
@@ -181,9 +181,10 @@
         ],
         axis=0,
     )
+    d_full = lax.psum(d_part, ("prow", "pcol"))
+    d_full, x_part, y_part = lax.optimization_barrier((d_full, x_part, y_part))
     x_full = lax.psum(x_part, "pcol")
     y_full = lax.psum(y_part, "prow")
-    d_full = lax.psum(d_part, ("prow", "pcol"))
     low = jnp.tril(jnp.linalg.cholesky(d_full))
     low_inv = jax.scipy.linalg.solve_triangular(
         low, jnp.eye(panel, dtype=jnp.float32), lower=True

time: 935 us -> 838 us (0.90)
  waiting for transfers between devices: 168 us -> 84.4 us
  local copies, waits for them, and re-layouts: 213 us -> 188 us
  matrix products: 148 us -> 159 us
  other arithmetic: 352 us -> 363 us
    psum x1, waiting for transfers between devices: 54.1 us -> 0.02 us  [local(): x_full = lax.psum(x_part, 'pcol')]
    psum x1, waiting for transfers between devices: 81.2 us -> 29.5 us  [local(): d_full = lax.psum(d_part, ('prow', 'pcol'))]
    reshape x2 -> x1, local copies, waits for them, and re-layouts: 31.3 us -> 13.5 us  [local(): return matrix.reshape(front.shape)]
    all_to_all x1, waiting for transfers between devices: 32.5 us -> 48.5 us  [local(): lax.all_to_all(staged.reshape(child_rows, grid_cols, cap_cols), 'pcol', s...]
    dot_general x1, matrix products: 17.7 us -> 31 us  [local(): lax.dot_general(y_full, low_inv, (((0,), (1,)), ((), ())), precision=HIGH...]
    gather x2 -> x3, local copies, waits for them, and re-layouts: 28.5 us -> 37.8 us  [local(): added = jnp.take(jnp.take(arrived, row_recv, axis=0), col_recv, axis=1)]
    another operation x40 -> x24, local copies, waits for them, and re-layouts: 24.5 us -> 22.2 us
where the time goes in v4:
time: 838 us; the launch traced here: 831 us
  other arithmetic  363 us (43%)
  local copies, waits for them, and re-layouts  188 us (22%)
  matrix products  159 us (19%)
  waiting for transfers between devices  84.4 us (10%)
  between operations  19.2 us (2%)
  starting transfers between devices  16.4 us (2%)
    another operation x31, other arithmetic, local(): low = jnp.tril(jnp.linalg.cholesky(d_full))  173 us
    another operation x3, other arithmetic, local(): jax.scipy.linalg.solve_triangular(low, jnp.eye(panel, dtype=jnp.float32),...  85.8 us
    all_to_all x1, waiting for transfers between devices, local(): lax.all_to_all(staged.reshape(child_rows, grid_cols, cap_cols), 'pcol', s...  48.5 us
    gather x3, local copies, waits for them, and re-layouts, local(): added = jnp.take(jnp.take(arrived, row_recv, axis=0), col_recv, axis=1)  37.8 us
    dot_general x1, matrix products, local(): matrix = matrix - jnp.dot(rows_u, cols_u.T, precision=HIGHEST)  35.2 us
    dot_general x1, matrix products, local(): rows_f = jnp.dot(x_full, low_inv.T, precision=HIGHEST)  31.1 us
    dot_general x1, matrix products, local(): lax.dot_general(y_full, low_inv, (((0,), (1,)), ((), ())), precision=HIGH...  31 us
    psum x1, waiting for transfers between devices, local(): d_full = lax.psum(d_part, ('prow', 'pcol'))  29.5 us
  transfers between devices with their start and end apart: 5, of which 3 were waited for; matrix products, arithmetic and copies ran while one was open for 49% of the time, Pallas kernels for 0%

profile of v4, /device:TPU:1, one launch (start us, length us, event | category | flops | bytes accessed | tf_op | source)
XLA Modules:
  0.0 831.1 jit_solution(5883725917562887210)
XLA Ops:
  44.1 48.5 %all-to-all-done = f32[1024,16,64]{0,2,1:T(8,128)} async-done(((f32[1024,16,64]{0,2,1:T(8,128)}), f32[1024,16,64]{0,2,1:T(8,128)}, u32[]{:S(2)}, u32[]{:S(2)}) %all-to-all-start) | async-done | bytes 4194336 | tf_op jit(solution)/shard_map/all_to_all | solution.py:132
  102.6 13.8 %gather_fusion.3 = f32[2048,1024]{1,0:T(8,128)} fusion(f32[1025,1024]{1,0:T(8,128)} %pad.14, s32[2048]{0:T(1024)S(1)} %broadcast_clamp_fusion), kind=kCustom, calls=%fused_computation.3 | custom fusion | bytes 16785408 | tf_op jit(solution)/shard_map/jit(_take)/gather | solution.py:135
  159.7 13.0 %gather_fusion.7 = s32[2048]{0:T(1024)S(1)} fusion(s32[8,1024]{1,0:T(8,128)S(1)} %bitcast.161, s32[2048]{0:T(1024)S(1)} %bitcast.162), kind=kCustom, calls=%fused_computation.7 | custom fusion | bytes 32768 | tf_op jit(solution)/shard_map/jit(take_along_axis)/gather | solution.py:55
  173.1 29.2 %reduce.84 = f32[4,512,2,512]{3,2,1,0:T(2,128)} reduce(f32[4,1,512,2,1,512]{5,4,3,2,1,0:T(1,128)} %param.3, f32[]{:T(128)} %constant.634), dimensions={1,4}, to_apply=%param.3.reduce_sub_computation | reduce | bytes 16777220 | tf_op args[0]
  238.5 16.3 %gather_fusion.4 = f32[2048,1025]{1,0:T(8,128)} fusion(f32[2049,1025]{1,0:T(8,128)} %pad.15, s32[2048]{0:T(1024)S(1)} %fusion.120), kind=kCustom, calls=%fused_computation.4 | custom fusion | bytes 16801792 | tf_op jit(solution)/shard_map/jit(_take)/gather | solution.py:140
  272.3 12.3 %gather_fusion.5 = f32[1024,2048]{1,0:T(8,128)} fusion(f32[2048,1025]{0,1:T(8,128)} %copy.49, s32[1024]{0:T(1024)S(1)} %get-tuple-element.107), kind=kCustom, calls=%fused_computation.5 | custom fusion | bytes 16781312 | tf_op jit(solution)/shard_map/jit(_take)/gather | solution.py:140
  293.9 12.3 %bitcast_add_fusion = f32[2048,1024]{1,0:T(8,128)} fusion(f32[2048,1024]{1,0:T(8,128)} %bitcast.165, f32[1024,2048]{0,1:T(8,128)} %copy.50, pred[1024]{0:T(1024)(128)(4,1)S(1)} %compare_and_fusion.5), kind=kLoop, calls=%fused_computation.22 | loop fusion | flops 4194304 | bytes 25166848 | tf_op jit(solution)/shard_map/add | solution.py:141
  318.7 29.5 %all-reduce.8.cloned.1.call-done = f32[1024,1024]{0,1:T(8,128)} async-done(((f32[1024,1024]{0,1:T(8,128)}), f32[1024,1024]{0,1:T(8,128)}) %all-reduce.8.cloned.1.call-update) | async-done | bytes 4194320 | tf_op jit(solution)/shard_map/psum | solution.py:184
  360.3 11.7 %cholesky.222 = f32[128,128]{1,0:T(8,128)S(1)} custom-call(f32[128,128]{1,0:T(8,128)S(1)} %cholesky.577), custom_call_target="Cholesky" | custom-call | tf_op jit(solution)/shard_map/jit(cholesky)/cholesky | solution.py:188
  388.3 11.9 %cholesky.243 = f32[128,128]{1,0:T(8,128)S(1)} custom-call(f32[128,128]{1,0:T(8,128)S(1)} %cholesky.581), custom_call_target="Cholesky" | custom-call | tf_op jit(solution)/shard_map/jit(cholesky)/cholesky | solution.py:188
  400.8 9.8 %custom-call.64 = f32[1,128,128]{1,2,0:T(8,128)S(1)} custom-call(f32[1,128,128]{2,1,0:T(8,128)S(1)} %get-tuple-element.92), custom_call_target="InvertDiagBlocksLowerTriangular" | custom-call | tf_op jit(solution)/shard_map/jit(cholesky)/cholesky | solution.py:188
  414.0 11.7 %cholesky.466 = f32[128,128]{1,0:T(8,128)S(1)} custom-call(f32[128,128]{1,0:T(8,128)S(1)} %cholesky.586), custom_call_target="Cholesky" | custom-call | tf_op jit(solution)/shard_map/jit(cholesky)/cholesky | solution.py:188
  439.7 11.9 %cholesky.485 = f32[128,128]{1,0:T(8,128)S(1)} custom-call(f32[128,128]{1,0:T(8,128)S(1)} %cholesky.591), custom_call_target="Cholesky" | custom-call | tf_op jit(solution)/shard_map/jit(cholesky)/cholesky | solution.py:188
  465.6 11.7 %cholesky.504 = f32[128,128]{1,0:T(8,128)S(1)} custom-call(f32[128,128]{1,0:T(8,128)S(1)} %cholesky.596), custom_call_target="Cholesky" | custom-call | tf_op jit(solution)/shard_map/jit(cholesky)/cholesky | solution.py:188
  478.0 10.2 %custom-call.67 = f32[1,128,128]{1,2,0:T(8,128)S(1)} custom-call(f32[1,128,128]{2,1,0:T(8,128)S(1)} %get-tuple-element.83), custom_call_target="InvertDiagBlocksLowerTriangular" | custom-call | tf_op jit(solution)/shard_map/jit(cholesky)/cholesky | solution.py:188
  491.5 11.7 %cholesky.524 = f32[128,128]{1,0:T(8,128)S(1)} custom-call(f32[128,128]{1,0:T(8,128)S(1)} %cholesky.601), custom_call_target="Cholesky" | custom-call | tf_op jit(solution)/shard_map/jit(cholesky)/cholesky | solution.py:188
  516.9 11.7 %cholesky.544 = f32[128,128]{1,0:T(8,128)S(1)} custom-call(f32[128,128]{1,0:T(8,128)S(1)} %cholesky.606), custom_call_target="Cholesky" | custom-call | tf_op jit(solution)/shard_map/jit(cholesky)/cholesky | solution.py:188
  541.7 11.7 %cholesky.562 = f32[128,128]{1,0:T(8,128)S(1)} custom-call(f32[128,128]{1,0:T(8,128)S(1)} %convolution_subtract_fusion.11), custom_call_target="Cholesky" | custom-call | tf_op jit(solution)/shard_map/jit(cholesky)/cholesky | solution.py:188
  571.0 22.4 %while.1 = (s32[]{:T(128)}, f32[1024,1024]{1,0:T(8,128)}, s32[8,2]{0,1:T(2,128)S(1)}, f32[8,128,128]{2,1,0:T(8,128)S(1)}, s32[]{:T(128)}) while((s32[]{:T(128)}, f32[1024,1024]{1,0:T(8,128)}, s32[8,2]{0,1:T(2,128)S(1)}, f32[8,128,128]{2,1,0:T(8,128)S(1)}, s32[]{:T(128)}) %tuple.76), condition=%wide.while_cond, body=%wide.while_body.sunk | while | flops 2 | bytes 131181 | solution.py:189
  593.4 79.0 %custom-call.70 = f32[8,128,128]{1,2,0:T(8,128)S(1)} custom-call(f32[8,128,128]{2,1,0:T(8,128)S(1)} %get-tuple-element.22), custom_call_target="InvertDiagBlocksLowerTriangular" | custom-call | tf_op jit(solution)/shard_map/jit(_solve_triangular)/triangular_solve | solution.py:189
  700.8 31.0 %fusion.147 = f32[1024,1024]{1,0:T(8,128)} fusion(f32[1024,1024]{1,0:T(8,128)} %all-reduce.12.cloned.1.call-done, f32[1024,1024]{1,0:T(8,128)} %convolution_dynamic-update-slice_fusion), kind=kOutput, calls=%fused_computation.367 | convolution fusion | flops 12884901888 | bytes 12582912 | tf_op jit(solution)/shard_map/dot_general | solution.py:193
  731.8 31.1 %fusion.146 = f32[2048,1024]{1,0:T(8,128)S(1)} fusion(f32[2048,1024]{1,0:T(8,128)} %all-reduce.10.cloned.1.call-done, f32[1024,1024]{1,0:T(8,128)} %convolution_dynamic-update-slice_fusion), kind=kOutput, calls=%fused_computation.366 | convolution fusion | flops 25769803776 | bytes 20971520 | tf_op jit(solution)/shard_map/dot_general | solution.py:192
  766.6 35.2 %fusion.18 = f32[2048,1024]{1,0:T(8,128)} fusion(f32[2048,1024]{1,0:T(8,128)} %bitcast_add_fusion, f32[1024,1024]{1,0:T(8,128)S(1)} %copy-done.6, f32[1536,1024]{1,0:T(8,128)S(1)} %slice.320, f32[512,1024]{1,0:T(8,128)S(1)} %slice_select_fusion.2, s32[2048]{0:T(1024)S(1)} %bitcast.175, pred[2048]{0:T(1024)(128)(4,1)S(1)} %bitcast.176, ...), kind=kOutput, calls=%fused_computation.48 | convolution fusion | flops 25781338112 | bytes 29371392 | tf_op jit(solution)/shard_map/dot_general | solution.py:203
  810.6 13.5 %reshape.791 = f32[4,1,512,2,1,512]{5,4,3,2,1,0:T(1,128)} reshape(f32[2048,1024]{1,0:T(8,128)} %pad_maximum_fusion.2) | data formatting | bytes 16777216 | tf_op jit(solution)/shard_map/reshape | solution.py:210
  (248 shorter events, 333.1 us)
Async XLA Ops:
  10.4 2.4 copy-start.4
  24.5 7.8 copy-start
  24.5 68.1 %all-to-all-start = ((f32[1024,16,64]{0,2,1:T(8,128)}), f32[1024,16,64]{0,2,1:T(8,128)}, u32[]{:S(2)}, u32[]{:S(2)}) async-start(f32[1024,16,64]{0,2,1:T(8,128)} %broadcast_select_fusion.2), calls=%async_computation | async-start | bytes 8388608 | tf_op jit(solution)/shard_map/all_to_all | solution.py:132
  122.2 108.3 %all-to-all-start.1 = ((f32[8,256,1024]{2,1,0:T(8,128)}), f32[8,256,1024]{2,1,0:T(8,128)}, u32[]{:S(2)}, u32[]{:S(2)}) async-start(f32[8,256,1024]{2,1,0:T(8,128)} %broadcast_select_fusion.1), calls=%async_computation.1 | async-start | bytes 16777216 | tf_op jit(solution)/shard_map/all_to_all | solution.py:136
  130.0 218.2 %all-reduce.8.cloned.1.call-start = ((), (), s32[]{:S(2)}) async-start(), calls=%async_computation.2 | async-start | bytes 8388608 | tf_op jit(solution)/shard_map/psum | solution.py:184
  136.1 11.7 %copy-start.5 = (f32[2,1,512,1,1,512]{5,2,3,4,1,0:T(8,128)S(1)}, f32[2,1,512,1,1,512]{5,2,3,4,1,0:T(8,128)}, u32[]{:S(2)}) copy-start(f32[2,1,512,1,1,512]{5,2,3,4,1,0:T(8,128)} %copy-done.4) | copy-start | bytes 6291460
  158.7 542.1 %all-reduce.12.cloned.1.call-start = ((), (), s32[]{:S(2)}) async-start(), calls=%async_computation.4 | async-start | bytes 8388608 | tf_op jit(solution)/shard_map/psum | solution.py:187
  358.3 2.0 copy-start.2
  513.7 218.1 %all-reduce.10.cloned.1.call-start = ((), (), s32[]{:S(2)}) async-start(), calls=%async_computation.3 | async-start | bytes 16777216 | tf_op jit(solution)/shard_map/psum | solution.py:186
  672.4 4.7 copy-start.1
  762.9 2.2 copy-start.3
  764.1 2.6 copy-start.6
Sparse Core Ops, SparseCore 0:
  158.8 189.3 all-reduce.7
  513.8 69.6 all-reduce.11
  587.0 142.7 all-reduce.9

commit v5 on v4

--- a/solution.py
+++ b/solution.py
@@ -102,6 +102,37 @@
                 diag_inverses[row_tile], partial_sum, precision=HIGHEST
             )
     return (jnp.block(low_tiles), jnp.block(inv_tiles))
+
+
+def lower_inverse(low, tile):
+    order = low.shape[0]
+    count = order // tile
+    diag = jnp.stack([low[k * tile : (k + 1) * tile, k * tile : (k + 1) * tile] for k in range(count)])
+    eye = jnp.broadcast_to(jnp.eye(tile, dtype=low.dtype), diag.shape)
+    inv = jax.scipy.linalg.solve_triangular(diag, eye, lower=True)
+    size = tile
+    while size < order:
+        pairs = inv.shape[0] // 2
+        upper = inv[0::2]
+        lower = inv[1::2]
+        off = jnp.stack(
+            [
+                low[(2 * p + 1) * size : (2 * p + 2) * size, 2 * p * size : (2 * p + 1) * size]
+                for p in range(pairs)
+            ]
+        )
+        mixed = -jnp.einsum(
+            "pij,pjk->pik",
+            jnp.einsum("pij,pjk->pik", lower, off, precision=HIGHEST),
+            upper,
+            precision=HIGHEST,
+        )
+        zero = jnp.zeros_like(upper)
+        top = jnp.concatenate([upper, zero], axis=2)
+        bottom = jnp.concatenate([mixed, lower], axis=2)
+        inv = jnp.concatenate([top, bottom], axis=1)
+        size *= 2
+    return inv[0]
 
 
 def local(front, child_block, child_to_parent):
@@ -186,9 +217,7 @@
     x_full = lax.psum(x_part, "pcol")
     y_full = lax.psum(y_part, "prow")
     low = jnp.tril(jnp.linalg.cholesky(d_full))
-    low_inv = jax.scipy.linalg.solve_triangular(
-        low, jnp.eye(panel, dtype=jnp.float32), lower=True
-    )
+    low_inv = lower_inverse(low, min(128, panel))
     rows_f = jnp.dot(x_full, low_inv.T, precision=HIGHEST)
     cols_f = lax.dot_general(
         y_full, low_inv, (((0,), (1,)), ((), ())), precision=HIGHEST

time: 838 us -> 793 us (0.946)
  matrix products: 159 us -> 136 us
  local copies, waits for them, and re-layouts: 188 us -> 171 us
    another operation x15 -> x1, matrix products: 28.3 us -> 0.99 us  [lower_inverse(): inv = jax.scipy.linalg.solve_triangular(diag, eye, lower=True)]
    another operation x25 -> x3, local copies, waits for them, and re-layouts: 22.2 us -> 2.04 us  [the longest x2 2.03 us: lower_inverse(): jnp.stack([low[(2 * p + 1) * size:(2 * p + 2) * size, 2 * p * size:(2 * p...]
    another operation x3 -> x2, other arithmetic: 85.8 us -> 78.8 us  [lower_inverse(): inv = jax.scipy.linalg.solve_triangular(diag, eye, lower=True)]
    unnamed x23 -> x30, local copies, waits for them, and re-layouts: 17.2 us -> 19.7 us
    another operation x31 -> x32, other arithmetic: 173 us -> 173 us  [local(): low = jnp.tril(jnp.linalg.cholesky(d_full))]
    unnamed x4 -> x3, other arithmetic: 29.3 us -> 29.3 us
  transfers between devices with their start and end apart: 5 -> 5, of which waited for: 3 -> 3; matrix products, arithmetic and copies ran while one was open for 49% -> 55% of each run, Pallas kernels for 0% -> 0%
where the time goes in v5:
time: 793 us; the launch traced here: 786 us
  other arithmetic  356 us (45%)
  local copies, waits for them, and re-layouts  171 us (22%)
  matrix products  136 us (17%)
  waiting for transfers between devices  87 us (11%)
  between operations  19.1 us (2%)
  starting transfers between devices  16.4 us (2%)
    another operation x32, other arithmetic, local(): low = jnp.tril(jnp.linalg.cholesky(d_full))  173 us
    another operation x2, other arithmetic, lower_inverse(): inv = jax.scipy.linalg.solve_triangular(diag, eye, lower=True)  78.8 us
    all_to_all x1, waiting for transfers between devices, local(): lax.all_to_all(staged.reshape(child_rows, grid_cols, cap_cols), 'pcol', s...  48.6 us
    gather x3, local copies, waits for them, and re-layouts, local(): added = jnp.take(jnp.take(arrived, row_recv, axis=0), col_recv, axis=1)  37.6 us
    dot_general x1, matrix products, local(): matrix = matrix - jnp.dot(rows_u, cols_u.T, precision=HIGHEST)  34.9 us
    dot_general x1, matrix products, local(): rows_f = jnp.dot(x_full, low_inv.T, precision=HIGHEST)  30 us
    dot_general x1, matrix products, local(): lax.dot_general(y_full, low_inv, (((0,), (1,)), ((), ())), precision=HIGH...  29.7 us
    unnamed x3, other arithmetic  29.3 us
  transfers between devices with their start and end apart: 5, of which 3 were waited for; matrix products, arithmetic and copies ran while one was open for 55% of the time, Pallas kernels for 0%

profile of v5, /device:TPU:1, one launch (start us, length us, event | category | flops | bytes accessed | tf_op | source)
XLA Modules:
  0.0 786.0 jit_solution(101313236435945438)
XLA Ops:
  44.0 48.6 %all-to-all-done = f32[1024,16,64]{0,2,1:T(8,128)} async-done(((f32[1024,16,64]{0,2,1:T(8,128)}), f32[1024,16,64]{0,2,1:T(8,128)}, u32[]{:S(2)}, u32[]{:S(2)}) %all-to-all-start) | async-done | bytes 4194336 | tf_op jit(solution)/shard_map/all_to_all | solution.py:163
  102.6 13.8 %gather_fusion.3 = f32[2048,1024]{1,0:T(8,128)} fusion(f32[1025,1024]{1,0:T(8,128)} %pad.17, s32[2048]{0:T(1024)S(1)} %broadcast_clamp_fusion), kind=kCustom, calls=%fused_computation.3 | custom fusion | bytes 16785408 | tf_op jit(solution)/shard_map/jit(_take)/gather | solution.py:166
  159.7 13.0 %gather_fusion.7 = s32[2048]{0:T(1024)S(1)} fusion(s32[8,1024]{1,0:T(8,128)S(1)} %bitcast.162, s32[2048]{0:T(1024)S(1)} %bitcast.163), kind=kCustom, calls=%fused_computation.7 | custom fusion | bytes 32768 | tf_op jit(solution)/shard_map/jit(take_along_axis)/gather | solution.py:55
  173.1 29.2 %reduce.84 = f32[4,512,2,512]{3,2,1,0:T(2,128)} reduce(f32[4,1,512,2,1,512]{5,4,3,2,1,0:T(1,128)} %param.3, f32[]{:T(128)} %constant.626), dimensions={1,4}, to_apply=%param.3.reduce_sub_computation | reduce | bytes 16777220 | tf_op args[0]
  238.5 16.1 %gather_fusion.4 = f32[2048,1025]{1,0:T(8,128)} fusion(f32[2049,1025]{1,0:T(8,128)} %pad.18, s32[2048]{0:T(1024)S(1)} %fusion.118), kind=kCustom, calls=%fused_computation.4 | custom fusion | bytes 16801792 | tf_op jit(solution)/shard_map/jit(_take)/gather | solution.py:171
  272.1 12.3 %gather_fusion.5 = f32[1024,2048]{1,0:T(8,128)} fusion(f32[2048,1025]{0,1:T(8,128)} %copy.67, s32[1024]{0:T(1024)S(1)} %get-tuple-element.70), kind=kCustom, calls=%fused_computation.5 | custom fusion | bytes 16781312 | tf_op jit(solution)/shard_map/jit(_take)/gather | solution.py:171
  293.7 12.3 %bitcast_add_fusion = f32[2048,1024]{1,0:T(8,128)} fusion(f32[2048,1024]{1,0:T(8,128)} %bitcast.166, f32[1024,2048]{0,1:T(8,128)} %copy.68, pred[1024]{0:T(1024)(128)(4,1)S(1)} %compare_and_fusion.5), kind=kLoop, calls=%fused_computation.20 | loop fusion | flops 4194304 | bytes 25166848 | tf_op jit(solution)/shard_map/add | solution.py:172
  318.5 29.2 %all-reduce.11.cloned.1.call-done = f32[1024,1024]{0,1:T(8,128)} async-done(((f32[1024,1024]{0,1:T(8,128)}), f32[1024,1024]{0,1:T(8,128)}) %all-reduce.11.cloned.1.call-update) | async-done | bytes 4194320 | tf_op jit(solution)/shard_map/psum | solution.py:215
  359.9 11.7 %cholesky.228 = f32[128,128]{1,0:T(8,128)S(1)} custom-call(f32[128,128]{1,0:T(8,128)S(1)} %cholesky.589), custom_call_target="Cholesky" | custom-call | tf_op jit(solution)/shard_map/jit(cholesky)/cholesky | solution.py:219
  374.1 9.8 %custom-call.63 = f32[1,128,128]{1,2,0:T(8,128)S(1)} custom-call(f32[1,128,128]{2,1,0:T(8,128)S(1)} %get-tuple-element.62), custom_call_target="InvertDiagBlocksLowerTriangular" | custom-call | tf_op jit(solution)/shard_map/jit(cholesky)/cholesky | solution.py:219
  387.8 11.9 %cholesky.249 = f32[128,128]{1,0:T(8,128)S(1)} custom-call(f32[128,128]{1,0:T(8,128)S(1)} %cholesky.593), custom_call_target="Cholesky" | custom-call | tf_op jit(solution)/shard_map/jit(cholesky)/cholesky | solution.py:219
  400.3 9.8 %custom-call.64 = f32[1,128,128]{1,2,0:T(8,128)S(1)} custom-call(f32[1,128,128]{2,1,0:T(8,128)S(1)} %get-tuple-element.59), custom_call_target="InvertDiagBlocksLowerTriangular" | custom-call | tf_op jit(solution)/shard_map/jit(cholesky)/cholesky | solution.py:219
  413.5 11.7 %cholesky.478 = f32[128,128]{1,0:T(8,128)S(1)} custom-call(f32[128,128]{1,0:T(8,128)S(1)} %cholesky.598), custom_call_target="Cholesky" | custom-call | tf_op jit(solution)/shard_map/jit(cholesky)/cholesky | solution.py:219
  425.8 9.8 %custom-call.65 = f32[1,128,128]{1,2,0:T(8,128)S(1)} custom-call(f32[1,128,128]{2,1,0:T(8,128)S(1)} %get-tuple-element.56), custom_call_target="InvertDiagBlocksLowerTriangular" | custom-call | tf_op jit(solution)/shard_map/jit(cholesky)/cholesky | solution.py:219
  439.5 11.7 %cholesky.497 = f32[128,128]{1,0:T(8,128)S(1)} custom-call(f32[128,128]{1,0:T(8,128)S(1)} %cholesky.603), custom_call_target="Cholesky" | custom-call | tf_op jit(solution)/shard_map/jit(cholesky)/cholesky | solution.py:219
  465.1 12.1 %cholesky.516 = f32[128,128]{1,0:T(8,128)S(1)} custom-call(f32[128,128]{1,0:T(8,128)S(1)} %cholesky.608), custom_call_target="Cholesky" | custom-call | tf_op jit(solution)/shard_map/jit(cholesky)/cholesky | solution.py:219
  491.0 11.7 %cholesky.536 = f32[128,128]{1,0:T(8,128)S(1)} custom-call(f32[128,128]{1,0:T(8,128)S(1)} %cholesky.613), custom_call_target="Cholesky" | custom-call | tf_op jit(solution)/shard_map/jit(cholesky)/cholesky | solution.py:219
  516.2 11.9 %cholesky.556 = f32[128,128]{1,0:T(8,128)S(1)} custom-call(f32[128,128]{1,0:T(8,128)S(1)} %cholesky.618), custom_call_target="Cholesky" | custom-call | tf_op jit(solution)/shard_map/jit(cholesky)/cholesky | solution.py:219
  541.1 11.7 %cholesky.574 = f32[128,128]{1,0:T(8,128)S(1)} custom-call(f32[128,128]{1,0:T(8,128)S(1)} %convolution_subtract_fusion.6), custom_call_target="Cholesky" | custom-call | tf_op jit(solution)/shard_map/jit(cholesky)/cholesky | solution.py:219
  568.3 78.8 %custom-call.70 = f32[8,1,128,128]{2,3,1,0:T(8,128)S(1)} custom-call(f32[8,1,128,128]{3,2,1,0:T(8,128)S(1)} %broadcast_select_fusion.3), custom_call_target="InvertDiagBlocksLowerTriangular" | custom-call | tf_op jit(solution)/shard_map/jit(_solve_triangular)/vmap()/triangular_solve | solution.py:112
  657.9 29.7 %fusion.23 = f32[1024,1024]{1,0:T(8,128)} fusion(f32[1024,1024]{1,0:T(8,128)} %all-reduce.15.cloned.1.call-done, f32[1,512,512]{2,1,0:T(8,128)S(1)} %get-tuple-element.32, f32[1,512,512]{2,1,0:T(8,128)S(1)} %get-tuple-element.31, f32[1,512,512]{2,1,0:T(8,128)S(1)} %fusion.34), kind=kOutput, calls=%fused_computation.50 | convolution fusion | flops 12889096192 | bytes 11534336 | tf_op jit(solution)/shard_map/dot_general | solution.py:222
  687.6 30.0 %fusion.25 = f32[2048,1024]{1,0:T(8,128)S(1)} fusion(f32[2048,1024]{1,0:T(8,128)} %all-reduce.13.cloned.1.call-done, f32[1,512,512]{2,1,0:T(8,128)S(1)} %get-tuple-element.32, f32[1,512,512]{2,1,0:T(8,128)S(1)} %get-tuple-element.31, f32[1,512,512]{2,1,0:T(8,128)S(1)} %fusion.34), kind=kOutput, calls=%fused_computation.51 | convolution fusion | flops 25773998080 | bytes 19922944 | tf_op jit(solution)/shard_map/dot_general | solution.py:221
  722.0 34.9 %fusion.18 = f32[2048,1024]{1,0:T(8,128)} fusion(f32[2048,1024]{1,0:T(8,128)} %bitcast_add_fusion, f32[1024,1024]{1,0:T(8,128)S(1)} %copy-done.6, f32[1536,1024]{1,0:T(8,128)S(1)} %slice.349, f32[512,1024]{1,0:T(8,128)S(1)} %slice_select_fusion.2, s32[2048]{0:T(1024)S(1)} %bitcast.176, pred[2048]{0:T(1024)(128)(4,1)S(1)} %bitcast.177, ...), kind=kOutput, calls=%fused_computation.47 | convolution fusion | flops 25781338112 | bytes 29371392 | tf_op jit(solution)/shard_map/dot_general | solution.py:232
  765.7 13.5 %reshape.891 = f32[4,1,512,2,1,512]{5,4,3,2,1,0:T(1,128)} reshape(f32[2048,1024]{1,0:T(8,128)} %pad_maximum_fusion.2) | data formatting | bytes 16777216 | tf_op jit(solution)/shard_map/reshape | solution.py:239
  (228 shorter events, 281.8 us)
Async XLA Ops:
  10.4 2.4 copy-start.4
  24.5 7.8 copy-start
  24.5 68.1 %all-to-all-start = ((f32[1024,16,64]{0,2,1:T(8,128)}), f32[1024,16,64]{0,2,1:T(8,128)}, u32[]{:S(2)}, u32[]{:S(2)}) async-start(f32[1024,16,64]{0,2,1:T(8,128)} %broadcast_select_fusion.2), calls=%async_computation | async-start | bytes 8388608 | tf_op jit(solution)/shard_map/all_to_all | solution.py:163
  122.2 108.3 %all-to-all-start.1 = ((f32[8,256,1024]{2,1,0:T(8,128)}), f32[8,256,1024]{2,1,0:T(8,128)}, u32[]{:S(2)}, u32[]{:S(2)}) async-start(f32[8,256,1024]{2,1,0:T(8,128)} %broadcast_select_fusion.1), calls=%async_computation.1 | async-start | bytes 16777216 | tf_op jit(solution)/shard_map/all_to_all | solution.py:167
  130.0 217.7 %all-reduce.11.cloned.1.call-start = ((), (), s32[]{:S(2)}) async-start(), calls=%async_computation.2 | async-start | bytes 8388608 | tf_op jit(solution)/shard_map/psum | solution.py:215
  136.1 11.7 %copy-start.5 = (f32[2,1,512,1,1,512]{5,2,3,4,1,0:T(8,128)S(1)}, f32[2,1,512,1,1,512]{5,2,3,4,1,0:T(8,128)}, u32[]{:S(2)}) copy-start(f32[2,1,512,1,1,512]{5,2,3,4,1,0:T(8,128)} %copy-done.4) | copy-start | bytes 6291460
  158.6 499.3 %all-reduce.15.cloned.1.call-start = ((), (), s32[]{:S(2)}) async-start(), calls=%async_computation.4 | async-start | bytes 8388608 | tf_op jit(solution)/shard_map/psum | solution.py:218
  357.9 2.0 copy-start.3
  435.7 251.9 %all-reduce.13.cloned.1.call-start = ((), (), s32[]{:S(2)}) async-start(), calls=%async_computation.3 | async-start | bytes 16777216 | tf_op jit(solution)/shard_map/psum | solution.py:217
  566.3 2.0 copy-start.1
  717.6 2.2 copy-start.2
  719.8 2.2 copy-start.6
Sparse Core Ops, SparseCore 0:
  158.8 188.8 all-reduce.10
  435.8 69.6 all-reduce.14
  514.2 140.0 all-reduce.12

commit v6 on v5

--- a/solution.py
+++ b/solution.py
@@ -135,6 +135,42 @@
     return inv[0]
 
 
+def corner_part(front, child_local, child_to_parent, my_row, my_col, grid_rows, grid_cols):
+    block_width = front.shape[2]
+    child_rblocks = child_local.shape[0] // block_width
+    child_cblocks = child_local.shape[1] // block_width
+    panel = NP * block_width
+    panel_ids = jnp.arange(panel, dtype=jnp.int32)
+    child_row_ids = (
+        (jnp.arange(child_rblocks, dtype=jnp.int32)[:, None] * grid_rows + my_row) * block_width
+        + jnp.arange(block_width, dtype=jnp.int32)[None, :]
+    ).reshape(-1)
+    child_col_ids = (
+        (jnp.arange(child_cblocks, dtype=jnp.int32)[:, None] * grid_cols + my_col) * block_width
+        + jnp.arange(block_width, dtype=jnp.int32)[None, :]
+    ).reshape(-1)
+    row_hit = (child_to_parent[child_row_ids][None, :] == panel_ids[:, None]).astype(jnp.float32)
+    col_hit = (child_to_parent[child_col_ids][None, :] == panel_ids[:, None]).astype(jnp.float32)
+    corner_child = jnp.dot(
+        jnp.dot(row_hit, child_local, precision=HIGHEST), col_hit.T, precision=HIGHEST
+    )
+    corner = front[0, 0, :, 0, 0, :]
+    zero_corner = jnp.zeros_like(corner)
+    return corner_child + jnp.concatenate(
+        [
+            jnp.concatenate(
+                [
+                    jnp.where((my_row == p) & (my_col == q), corner, zero_corner)
+                    for q in range(NP)
+                ],
+                axis=1,
+            )
+            for p in range(NP)
+        ],
+        axis=0,
+    )
+
+
 def local(front, child_block, child_to_parent):
     grid_rows = lax.axis_size("prow")
     grid_cols = lax.axis_size("pcol")
@@ -163,13 +199,16 @@
     staged = lax.all_to_all(
         staged.reshape(child_rows, grid_cols, cap_cols), "pcol", split_axis=1, concat_axis=1, tiled=True
     ).reshape(child_rows, grid_cols * cap_cols)
+    front_mat = front.reshape(local_rows, local_cols)
+    d_part = corner_part(front, child_local, child_to_parent, my_row, my_col, grid_rows, grid_cols)
+    staged, d_part, front_mat = lax.optimization_barrier((staged, d_part, front_mat))
     moved = jnp.take(jnp.pad(staged, ((0, 1), (0, 0))), row_send, axis=0)
     moved = lax.all_to_all(
         moved.reshape(grid_rows, cap_rows, grid_cols * cap_cols), "prow", split_axis=0, concat_axis=0, tiled=True
     )
     arrived = jnp.pad(moved.reshape(grid_rows * cap_rows, grid_cols * cap_cols), ((0, 1), (0, 1)))
     added = jnp.take(jnp.take(arrived, row_recv, axis=0), col_recv, axis=1)
-    matrix = front.reshape(local_rows, local_cols) + added
+    matrix = front_mat + added
     panel = NP * block_width
     row_blk = jnp.repeat(jnp.arange(row_blocks, dtype=jnp.int32) * grid_rows + my_row, block_width)
     col_blk = jnp.repeat(jnp.arange(col_blocks, dtype=jnp.int32) * grid_cols + my_col, block_width)
@@ -183,35 +222,6 @@
     y_part = jnp.concatenate(
         [jnp.where(my_row == p, first_rows, zero_rows) for p in range(NP)], axis=0
     )
-    panel_ids = jnp.arange(panel, dtype=jnp.int32)
-    child_row_ids = (
-        (jnp.arange(child_rblocks, dtype=jnp.int32)[:, None] * grid_rows + my_row) * block_width
-        + jnp.arange(block_width, dtype=jnp.int32)[None, :]
-    ).reshape(-1)
-    child_col_ids = (
-        (jnp.arange(child_cblocks, dtype=jnp.int32)[:, None] * grid_cols + my_col) * block_width
-        + jnp.arange(block_width, dtype=jnp.int32)[None, :]
-    ).reshape(-1)
-    row_hit = (child_to_parent[child_row_ids][None, :] == panel_ids[:, None]).astype(jnp.float32)
-    col_hit = (child_to_parent[child_col_ids][None, :] == panel_ids[:, None]).astype(jnp.float32)
-    corner_child = jnp.dot(
-        jnp.dot(row_hit, child_local, precision=HIGHEST), col_hit.T, precision=HIGHEST
-    )
-    corner = front[0, 0, :, 0, 0, :]
-    zero_corner = jnp.zeros_like(corner)
-    d_part = corner_child + jnp.concatenate(
-        [
-            jnp.concatenate(
-                [
-                    jnp.where((my_row == p) & (my_col == q), corner, zero_corner)
-                    for q in range(NP)
-                ],
-                axis=1,
-            )
-            for p in range(NP)
-        ],
-        axis=0,
-    )
     d_full = lax.psum(d_part, ("prow", "pcol"))
     d_full, x_part, y_part = lax.optimization_barrier((d_full, x_part, y_part))
     x_full = lax.psum(x_part, "pcol")
@@ -229,13 +239,10 @@
     keep_row = (row_blk[:, None] >= NP) | (lane < (row_blk[:, None] * block_width))
     rows_u = jnp.where(keep_row, rows_f, 0.0)
     cols_u = jnp.where((col_blk >= NP)[:, None], cols_f, 0.0)
-    matrix = matrix - jnp.dot(rows_u, cols_u.T, precision=HIGHEST)
-    out_first = matrix[:, :block_width]
-    for p in range(NP):
-        out_first = jnp.where(
-            my_col == p, rows_f[:, p * block_width : (p + 1) * block_width], out_first
-        )
-    matrix = jnp.concatenate([out_first, matrix[:, block_width:]], axis=1)
+    updated = matrix - jnp.dot(rows_u, cols_u.T, precision=HIGHEST)
+    panel_src = jnp.where(my_col == 0, rows_f, jnp.roll(rows_f, -block_width, axis=1))
+    out_lane = jnp.arange(local_cols, dtype=jnp.int32)[None, :]
+    matrix = jnp.where((out_lane < block_width) & (my_col < NP), panel_src, updated)
     return matrix.reshape(front.shape)
 
 

time: 793 us -> 796 us (level)
    all_to_all x1, waiting for transfers between devices: 9.22 us -> 77.6 us  [local(): lax.all_to_all(moved.reshape(grid_rows, cap_rows, grid_cols * cap_cols),...]
    all_to_all x1, waiting for transfers between devices: 48.6 us -> 0.01 us  [local(): lax.all_to_all(staged.reshape(child_rows, grid_cols, cap_cols), 'pcol', s...]
    psum x1, waiting for transfers between devices: 29.2 us -> 13 us  [local(): d_full = lax.psum(d_part, ('prow', 'pcol'))]
    unnamed x30 -> x34, local copies, waits for them, and re-layouts: 19.7 us -> 20.7 us
    unnamed x3 -> x4, other arithmetic: 29.3 us -> 29.8 us
  transfers between devices with their start and end apart: 5 -> 5, of which waited for: 3 -> 2; matrix products, arithmetic and copies ran while one was open for 55% -> 55% of each run, Pallas kernels for 0% -> 0%
where the time goes in v6:
time: 796 us; the launch traced here: 786 us
  other arithmetic  352 us (44%)
  local copies, waits for them, and re-layouts  171 us (21%)
  matrix products  139 us (17%)
  waiting for transfers between devices  90.6 us (11%)
  between operations  19.2 us (2%)
  starting transfers between devices  14.4 us (2%)
    another operation x32, other arithmetic, local(): low = jnp.tril(jnp.linalg.cholesky(d_full))  173 us
    another operation x2, other arithmetic, lower_inverse(): inv = jax.scipy.linalg.solve_triangular(diag, eye, lower=True)  78.8 us
    all_to_all x1, waiting for transfers between devices, local(): lax.all_to_all(moved.reshape(grid_rows, cap_rows, grid_cols * cap_cols),...  77.6 us
    gather x3, local copies, waits for them, and re-layouts, local(): added = jnp.take(jnp.take(arrived, row_recv, axis=0), col_recv, axis=1)  37.7 us
    dot_general x1, matrix products, local(): updated = matrix - jnp.dot(rows_u, cols_u.T, precision=HIGHEST)  37.2 us
    dot_general x1, matrix products, local(): rows_f = jnp.dot(x_full, low_inv.T, precision=HIGHEST)  30.1 us
    unnamed x4, other arithmetic  29.8 us
    dot_general x1, matrix products, local(): lax.dot_general(y_full, low_inv, (((0,), (1,)), ((), ())), precision=HIGH...  29.7 us
  transfers between devices with their start and end apart: 5, of which 2 were waited for; matrix products, arithmetic and copies ran while one was open for 55% of the time, Pallas kernels for 0%

profile of v6, /device:TPU:1, one launch (start us, length us, event | category | flops | bytes accessed | tf_op | source)
XLA Modules:
  0.0 786.3 jit_solution(5794163786047271064)
XLA Ops:
  57.2 29.7 %reduce.84 = f32[4,512,2,512]{3,2,1,0:T(2,128)} reduce(f32[4,1,512,2,1,512]{5,4,3,2,1,0:T(1,128)} %param.3, f32[]{:T(128)} %constant.627), dimensions={1,4}, to_apply=%param.3.reduce_sub_computation | reduce | bytes 16777220 | tf_op args[0]
  118.9 13.8 %gather_fusion.3 = f32[2048,1024]{1,0:T(8,128)} fusion(f32[1025,1024]{1,0:T(8,128)} %pad.17, s32[2048]{0:T(1024)S(1)} %broadcast_clamp_fusion), kind=kCustom, calls=%fused_computation.3 | custom fusion | bytes 16785408 | tf_op jit(solution)/shard_map/jit(_take)/gather | solution.py:205
  145.5 13.0 %gather_fusion.7 = s32[2048]{0:T(1024)S(1)} fusion(s32[8,1024]{1,0:T(8,128)S(1)} %bitcast.162, s32[2048]{0:T(1024)S(1)} %bitcast.163), kind=kCustom, calls=%fused_computation.7 | custom fusion | bytes 32768 | tf_op jit(solution)/shard_map/jit(take_along_axis)/gather | solution.py:55
  169.4 77.6 %all-to-all-done.1 = f32[8,256,1024]{2,1,0:T(8,128)} async-done(((f32[8,256,1024]{2,1,0:T(8,128)}), f32[8,256,1024]{2,1,0:T(8,128)}, u32[]{:S(2)}, u32[]{:S(2)}) %all-to-all-start.1) | async-done | bytes 8388640 | tf_op jit(solution)/shard_map/all_to_all | solution.py:206
  255.0 16.1 %gather_fusion.4 = f32[2048,1025]{1,0:T(8,128)} fusion(f32[2049,1025]{1,0:T(8,128)} %pad.18, s32[2048]{0:T(1024)S(1)} %fusion.115), kind=kCustom, calls=%fused_computation.4 | custom fusion | bytes 16801792 | tf_op jit(solution)/shard_map/jit(_take)/gather | solution.py:210
  288.6 12.3 %gather_fusion.5 = f32[1024,2048]{1,0:T(8,128)} fusion(f32[2048,1025]{0,1:T(8,128)} %copy.64, s32[1024]{0:T(1024)S(1)} %get-tuple-element.78), kind=kCustom, calls=%fused_computation.5 | custom fusion | bytes 16781312 | tf_op jit(solution)/shard_map/jit(_take)/gather | solution.py:210
  310.1 12.2 %bitcast_add_fusion = f32[2048,1024]{1,0:T(8,128)} fusion(f32[2048,1024]{1,0:T(8,128)} %bitcast.166, f32[1024,2048]{0,1:T(8,128)} %copy.65, pred[1024]{0:T(1024)(128)(4,1)S(1)} %compare_and_fusion.5), kind=kLoop, calls=%fused_computation.19 | loop fusion | flops 4194304 | bytes 25166848 | tf_op jit(solution)/shard_map/add | solution.py:211
  335.1 13.0 %all-reduce.11.cloned.1.call-done = f32[1024,1024]{0,1:T(8,128)} async-done(((f32[1024,1024]{0,1:T(8,128)}), f32[1024,1024]{0,1:T(8,128)}) %all-reduce.11.cloned.1.call-update) | async-done | bytes 4194320 | tf_op jit(solution)/shard_map/psum | solution.py:225
  360.2 11.7 %cholesky.228 = f32[128,128]{1,0:T(8,128)S(1)} custom-call(f32[128,128]{1,0:T(8,128)S(1)} %cholesky.589), custom_call_target="Cholesky" | custom-call | tf_op jit(solution)/shard_map/jit(cholesky)/cholesky | solution.py:229
  374.5 9.8 %custom-call.63 = f32[1,128,128]{1,2,0:T(8,128)S(1)} custom-call(f32[1,128,128]{2,1,0:T(8,128)S(1)} %get-tuple-element.68), custom_call_target="InvertDiagBlocksLowerTriangular" | custom-call | tf_op jit(solution)/shard_map/jit(cholesky)/cholesky | solution.py:229
  388.2 11.9 %cholesky.249 = f32[128,128]{1,0:T(8,128)S(1)} custom-call(f32[128,128]{1,0:T(8,128)S(1)} %cholesky.593), custom_call_target="Cholesky" | custom-call | tf_op jit(solution)/shard_map/jit(cholesky)/cholesky | solution.py:229
  400.7 9.8 %custom-call.64 = f32[1,128,128]{1,2,0:T(8,128)S(1)} custom-call(f32[1,128,128]{2,1,0:T(8,128)S(1)} %get-tuple-element.65), custom_call_target="InvertDiagBlocksLowerTriangular" | custom-call | tf_op jit(solution)/shard_map/jit(cholesky)/cholesky | solution.py:229
  413.9 11.7 %cholesky.478 = f32[128,128]{1,0:T(8,128)S(1)} custom-call(f32[128,128]{1,0:T(8,128)S(1)} %cholesky.598), custom_call_target="Cholesky" | custom-call | tf_op jit(solution)/shard_map/jit(cholesky)/cholesky | solution.py:229
  439.8 11.7 %cholesky.497 = f32[128,128]{1,0:T(8,128)S(1)} custom-call(f32[128,128]{1,0:T(8,128)S(1)} %cholesky.603), custom_call_target="Cholesky" | custom-call | tf_op jit(solution)/shard_map/jit(cholesky)/cholesky | solution.py:229
  465.5 12.1 %cholesky.516 = f32[128,128]{1,0:T(8,128)S(1)} custom-call(f32[128,128]{1,0:T(8,128)S(1)} %cholesky.608), custom_call_target="Cholesky" | custom-call | tf_op jit(solution)/shard_map/jit(cholesky)/cholesky | solution.py:229
  478.2 9.8 %custom-call.67 = f32[1,128,128]{1,2,0:T(8,128)S(1)} custom-call(f32[1,128,128]{2,1,0:T(8,128)S(1)} %get-tuple-element.56), custom_call_target="InvertDiagBlocksLowerTriangular" | custom-call | tf_op jit(solution)/shard_map/jit(cholesky)/cholesky | solution.py:229
  491.4 11.7 %cholesky.536 = f32[128,128]{1,0:T(8,128)S(1)} custom-call(f32[128,128]{1,0:T(8,128)S(1)} %cholesky.613), custom_call_target="Cholesky" | custom-call | tf_op jit(solution)/shard_map/jit(cholesky)/cholesky | solution.py:229
  516.6 11.9 %cholesky.556 = f32[128,128]{1,0:T(8,128)S(1)} custom-call(f32[128,128]{1,0:T(8,128)S(1)} %cholesky.618), custom_call_target="Cholesky" | custom-call | tf_op jit(solution)/shard_map/jit(cholesky)/cholesky | solution.py:229
  541.5 11.7 %cholesky.574 = f32[128,128]{1,0:T(8,128)S(1)} custom-call(f32[128,128]{1,0:T(8,128)S(1)} %convolution_subtract_fusion.6), custom_call_target="Cholesky" | custom-call | tf_op jit(solution)/shard_map/jit(cholesky)/cholesky | solution.py:229
  568.7 78.8 %custom-call.70 = f32[8,1,128,128]{2,3,1,0:T(8,128)S(1)} custom-call(f32[8,1,128,128]{3,2,1,0:T(8,128)S(1)} %broadcast_select_fusion.3), custom_call_target="InvertDiagBlocksLowerTriangular" | custom-call | tf_op jit(solution)/shard_map/jit(_solve_triangular)/vmap()/triangular_solve | solution.py:112
  658.3 29.7 %fusion.16 = f32[1024,1024]{1,0:T(8,128)} fusion(f32[1024,1024]{1,0:T(8,128)} %all-reduce.15.cloned.1.call-done, f32[1,512,512]{2,1,0:T(8,128)S(1)} %get-tuple-element.38, f32[1,512,512]{2,1,0:T(8,128)S(1)} %get-tuple-element.37, f32[1,512,512]{2,1,0:T(8,128)S(1)} %fusion.31), kind=kOutput, calls=%fused_computation.48 | convolution fusion | flops 12889096192 | bytes 11534336 | tf_op jit(solution)/shard_map/dot_general | solution.py:232
  688.0 30.1 %fusion.18 = f32[2048,1024]{1,0:T(8,128)S(1)} fusion(f32[2048,1024]{1,0:T(8,128)} %all-reduce.13.cloned.1.call-done, f32[1,512,512]{2,1,0:T(8,128)S(1)} %get-tuple-element.38, f32[1,512,512]{2,1,0:T(8,128)S(1)} %get-tuple-element.37, f32[1,512,512]{2,1,0:T(8,128)S(1)} %fusion.31), kind=kOutput, calls=%fused_computation.49 | convolution fusion | flops 25773998080 | bytes 19922944 | tf_op jit(solution)/shard_map/dot_general | solution.py:231
  728.8 37.2 %fusion.1 = f32[2048,1024]{1,0:T(8,128)} fusion(f32[2048,512]{1,0:T(8,128)} %get-tuple-element.26, f32[2048,512]{1,0:T(8,128)} %get-tuple-element.25, f32[2048,1024]{1,0:T(8,128)S(1)} %bitcast.168, f32[1536,1024]{1,0:T(8,128)} %copy-done.1, f32[512,1024]{1,0:T(8,128)S(1)} %slice_select_fusion.2, pred[]{:T(512)S(6)} %eq.114, ...), kind=kOutput, calls=%fused_computation.18 | convolution fusion | flops 25789726720 | bytes 37761024 | tf_op jit(solution)/shard_map/dot_general | solution.py:242
  766.1 13.5 %reshape.898 = f32[4,1,512,2,1,512]{5,4,3,2,1,0:T(1,128)} reshape(f32[2048,1024]{1,0:T(8,128)} %fusion.1) | data formatting | bytes 16777216 | tf_op jit(solution)/shard_map/reshape | solution.py:246
  (233 shorter events, 266.4 us)
Async XLA Ops:
  10.3 2.4 copy-start.5
  24.3 84.5 %all-to-all-start = ((f32[1024,16,64]{0,2,1:T(8,128)}), f32[1024,16,64]{0,2,1:T(8,128)}, u32[]{:S(2)}, u32[]{:S(2)}) async-start(f32[1024,16,64]{0,2,1:T(8,128)} %broadcast_select_fusion.2), calls=%async_computation | async-start | bytes 8388608 | tf_op jit(solution)/shard_map/all_to_all | solution.py:199
  32.8 11.8 %copy-start = (s32[8192]{0:T(1024)S(1)}, s32[8192]{0:T(1024)}, u32[]{:S(2)}) copy-start(s32[8192]{0:T(1024)} %param.5) | copy-start | bytes 98308
  86.8 11.0 %copy-start.6 = (f32[2,1,512,1,1,512]{5,2,3,4,1,0:T(8,128)S(1)}, f32[2,1,512,1,1,512]{5,2,3,4,1,0:T(8,128)}, u32[]{:S(2)}) copy-start(f32[2,1,512,1,1,512]{5,2,3,4,1,0:T(8,128)} %copy-done.5) | copy-start | bytes 6291460
  138.7 108.3 %all-to-all-start.1 = ((f32[8,256,1024]{2,1,0:T(8,128)}), f32[8,256,1024]{2,1,0:T(8,128)}, u32[]{:S(2)}, u32[]{:S(2)}) async-start(f32[8,256,1024]{2,1,0:T(8,128)} %broadcast_select_fusion.1), calls=%async_computation.1 | async-start | bytes 16777216 | tf_op jit(solution)/shard_map/all_to_all | solution.py:206
  144.9 203.1 %all-reduce.11.cloned.1.call-start = ((), (), s32[]{:S(2)}) async-start(), calls=%async_computation.2 | async-start | bytes 8388608 | tf_op jit(solution)/shard_map/psum | solution.py:225
  169.1 489.3 %all-reduce.15.cloned.1.call-start = ((), (), s32[]{:S(2)}) async-start(), calls=%async_computation.4 | async-start | bytes 8388608 | tf_op jit(solution)/shard_map/psum | solution.py:228
  358.2 2.0 copy-start.4
  436.1 252.0 %all-reduce.13.cloned.1.call-start = ((), (), s32[]{:S(2)}) async-start(), calls=%async_computation.3 | async-start | bytes 16777216 | tf_op jit(solution)/shard_map/psum | solution.py:227
  566.7 2.0 copy-start.2
  718.1 2.2 copy-start.3
  720.3 7.2 copy-start.1
  720.3 7.2 slice-start
  720.7 8.1 %slice-start.1 = ((s8[8388608]{0:T(1024)(128)(4,1)}), s8[4194304]{0:T(1024)(128)(4,1)S(1)}, s32[]{:S(2)}) async-start(s8[8388608]{0:T(1024)(128)(4,1)} %bitcast.167), calls=%async_computation.6 | async-start | bytes 8388608
Sparse Core Ops, SparseCore 0:
  169.2 178.7 all-reduce.10
  436.2 69.6 all-reduce.14
  514.6 139.9 all-reduce.12

commit v7 on v6

--- a/solution.py
+++ b/solution.py
@@ -196,12 +196,14 @@
     )
     child_local = child_block.reshape(child_rows, child_cols)
     staged = jnp.take(jnp.pad(child_local, ((0, 0), (0, 1))), col_send, axis=1)
+    d_part = corner_part(front, child_local, child_to_parent, my_row, my_col, grid_rows, grid_cols)
+    staged, d_part = lax.optimization_barrier((staged, d_part))
+    d_full = lax.psum(d_part, ("prow", "pcol"))
     staged = lax.all_to_all(
         staged.reshape(child_rows, grid_cols, cap_cols), "pcol", split_axis=1, concat_axis=1, tiled=True
     ).reshape(child_rows, grid_cols * cap_cols)
     front_mat = front.reshape(local_rows, local_cols)
-    d_part = corner_part(front, child_local, child_to_parent, my_row, my_col, grid_rows, grid_cols)
-    staged, d_part, front_mat = lax.optimization_barrier((staged, d_part, front_mat))
+    staged, front_mat = lax.optimization_barrier((staged, front_mat))
     moved = jnp.take(jnp.pad(staged, ((0, 1), (0, 0))), row_send, axis=0)
     moved = lax.all_to_all(
         moved.reshape(grid_rows, cap_rows, grid_cols * cap_cols), "prow", split_axis=0, concat_axis=0, tiled=True
@@ -222,12 +224,24 @@
     y_part = jnp.concatenate(
         [jnp.where(my_row == p, first_rows, zero_rows) for p in range(NP)], axis=0
     )
-    d_full = lax.psum(d_part, ("prow", "pcol"))
-    d_full, x_part, y_part = lax.optimization_barrier((d_full, x_part, y_part))
+    tile = min(128, block_width)
+    low00 = jnp.tril(jnp.linalg.cholesky(d_full[:block_width, :block_width]))
+    inv00 = lower_inverse(low00, tile)
+    low00, inv00, d_full, x_part, y_part = lax.optimization_barrier((low00, inv00, d_full, x_part, y_part))
     x_full = lax.psum(x_part, "pcol")
     y_full = lax.psum(y_part, "prow")
-    low = jnp.tril(jnp.linalg.cholesky(d_full))
-    low_inv = lower_inverse(low, min(128, panel))
+    low10 = jnp.dot(d_full[block_width:panel, :block_width], inv00.T, precision=HIGHEST)
+    schur = d_full[block_width:panel, block_width:panel] - jnp.dot(low10, low10.T, precision=HIGHEST)
+    low11 = jnp.tril(jnp.linalg.cholesky(schur))
+    inv11 = lower_inverse(low11, tile)
+    inv10 = -jnp.dot(jnp.dot(inv11, low10, precision=HIGHEST), inv00, precision=HIGHEST)
+    zero_blk = jnp.zeros_like(low00)
+    low = jnp.concatenate(
+        [jnp.concatenate([low00, zero_blk], axis=1), jnp.concatenate([low10, low11], axis=1)], axis=0
+    )
+    low_inv = jnp.concatenate(
+        [jnp.concatenate([inv00, zero_blk], axis=1), jnp.concatenate([inv10, inv11], axis=1)], axis=0
+    )
     rows_f = jnp.dot(x_full, low_inv.T, precision=HIGHEST)
     cols_f = lax.dot_general(
         y_full, low_inv, (((0,), (1,)), ((), ())), precision=HIGHEST

time: 796 us -> 833 us (1.046)
  waiting for transfers between devices: 90.6 us -> 137 us
    psum x1, waiting for transfers between devices: 13 us -> 92.9 us  [local(): d_full = lax.psum(d_part, ('prow', 'pcol'))]
    all_to_all x1, waiting for transfers between devices: 77.6 us -> 0.01 us  [local(): lax.all_to_all(moved.reshape(grid_rows, cap_rows, grid_cols * cap_cols),...]
    psum x1, waiting for transfers between devices: 0.01 us -> 34.5 us  [local(): x_full = lax.psum(x_part, 'pcol')]
    another operation x14 -> x12, matrix products: 23.1 us -> 8.5 us  [the longest x6 6.62 us: local(): low11 = jnp.tril(jnp.linalg.cholesky(schur))]
    another operation x32 -> x31, other arithmetic: 173 us -> 160 us  [the longest x15 80.9 us: local(): low11 = jnp.tril(jnp.linalg.cholesky(schur))]
    dot_general x0 -> x4, matrix products: none -> 9.89 us  [the longest x1 3.1 us: local(): jnp.dot(low10, low10.T, precision=HIGHEST)]
    all_to_all x1, waiting for transfers between devices: 0.01 us -> 8.51 us  [local(): lax.all_to_all(staged.reshape(child_rows, grid_cols, cap_cols), 'pcol', s...]
    unnamed x34 -> x43, local copies, waits for them, and re-layouts: 20.7 us -> 19.3 us
  transfers between devices with their start and end apart: 5 -> 5, of which waited for: 2 -> 3; matrix products, arithmetic and copies ran while one was open for 55% -> 49% of each run, Pallas kernels for 0% -> 0%
where the time goes in v7:
time: 833 us; the launch traced here: 817 us
  other arithmetic  347 us (42%)
  local copies, waits for them, and re-layouts  164 us (20%)
  waiting for transfers between devices  137 us (16%)
  matrix products  134 us (16%)
  between operations  19.3 us (2%)
  starting transfers between devices  15.9 us (2%)
    psum x1, waiting for transfers between devices, local(): d_full = lax.psum(d_part, ('prow', 'pcol'))  92.9 us
    another operation x15, other arithmetic, local(): low11 = jnp.tril(jnp.linalg.cholesky(schur))  80.9 us
    another operation x4, other arithmetic, lower_inverse(): inv = jax.scipy.linalg.solve_triangular(diag, eye, lower=True)  79.7 us
    another operation x16, other arithmetic, local(): low00 = jnp.tril(jnp.linalg.cholesky(d_full[:block_width, :block_width]))  79.4 us
    gather x3, local copies, waits for them, and re-layouts, local(): added = jnp.take(jnp.take(arrived, row_recv, axis=0), col_recv, axis=1)  37.5 us
    dot_general x1, matrix products, local(): updated = matrix - jnp.dot(rows_u, cols_u.T, precision=HIGHEST)  37.2 us
    psum x1, waiting for transfers between devices, local(): x_full = lax.psum(x_part, 'pcol')  34.5 us
    dot_general x1, matrix products, local(): rows_f = jnp.dot(x_full, low_inv.T, precision=HIGHEST)  30.4 us
  transfers between devices with their start and end apart: 5, of which 3 were waited for; matrix products, arithmetic and copies ran while one was open for 49% of the time, Pallas kernels for 0%

profile of v7, /device:TPU:1, one launch (start us, length us, event | category | flops | bytes accessed | tf_op | source)
XLA Modules:
  0.0 817.4 jit_solution(5939767482789415278)
XLA Ops:
  72.4 29.2 %reduce.52 = f32[4,512,2,512]{3,2,1,0:T(2,128)} reduce(f32[4,1,512,2,1,512]{5,4,3,2,1,0:T(1,128)} %param.6, f32[]{:T(128)} %constant.464), dimensions={1,4}, to_apply=%param.6.reduce_sub_computation | reduce | bytes 16777220 | tf_op args[0]
  111.5 13.0 %gather_fusion.7 = s32[2048]{0:T(1024)S(1)} fusion(s32[8,1024]{1,0:T(8,128)S(1)} %bitcast.167, s32[2048]{0:T(1024)S(1)} %bitcast.168), kind=kCustom, calls=%fused_computation.7 | custom fusion | bytes 32768 | tf_op jit(solution)/shard_map/jit(take_along_axis)/gather | solution.py:55
  145.9 13.8 %gather_fusion.3 = f32[2048,1024]{1,0:T(8,128)} fusion(f32[1025,1024]{1,0:T(8,128)} %pad.20, s32[2048]{0:T(1024)S(1)} %broadcast_clamp_fusion), kind=kCustom, calls=%fused_computation.3 | custom fusion | bytes 16785408 | tf_op jit(solution)/shard_map/jit(_take)/gather | solution.py:207
  181.6 92.9 %all-reduce.14.cloned.1.call-done = f32[1024,1024]{0,1:T(8,128)} async-done(((f32[1024,1024]{0,1:T(8,128)}), f32[1024,1024]{0,1:T(8,128)}) %all-reduce.14.cloned.1.call-update) | async-done | bytes 4194320 | tf_op jit(solution)/shard_map/psum | solution.py:201
  277.5 11.7 %cholesky.286 = f32[128,128]{1,0:T(8,128)S(1)} custom-call(f32[128,128]{1,0:T(8,128)S(1)} %cholesky.426), custom_call_target="Cholesky" | custom-call | tf_op jit(solution)/shard_map/jit(cholesky)/cholesky | solution.py:228
  289.4 9.9 %custom-call.31 = f32[1,128,128]{1,2,0:T(8,128)S(1)} custom-call(f32[1,128,128]{2,1,0:T(8,128)S(1)} %get-tuple-element.82), custom_call_target="InvertDiagBlocksLowerTriangular" | custom-call | tf_op jit(solution)/shard_map/jit(cholesky)/cholesky | solution.py:228
  300.0 11.7 %cholesky.305 = f32[128,128]{1,0:T(8,128)S(1)} custom-call(f32[128,128]{1,0:T(8,128)S(1)} %cholesky.430), custom_call_target="Cholesky" | custom-call | tf_op jit(solution)/shard_map/jit(cholesky)/cholesky | solution.py:228
  322.3 11.9 %cholesky.326 = f32[128,128]{1,0:T(8,128)S(1)} custom-call(f32[128,128]{1,0:T(8,128)S(1)} %cholesky.435), custom_call_target="Cholesky" | custom-call | tf_op jit(solution)/shard_map/jit(cholesky)/cholesky | solution.py:228
  344.6 11.7 %cholesky.343 = f32[128,128]{1,0:T(8,128)S(1)} custom-call(f32[128,128]{1,0:T(8,128)S(1)} %convolution_subtract_fusion.6), custom_call_target="Cholesky" | custom-call | tf_op jit(solution)/shard_map/jit(cholesky)/cholesky | solution.py:228
  361.7 39.7 %custom-call.34 = f32[4,1,128,128]{2,3,1,0:T(8,128)S(1)} custom-call(f32[4,1,128,128]{3,2,1,0:T(8,128)S(1)} %fusion.46), custom_call_target="InvertDiagBlocksLowerTriangular" | custom-call | tf_op jit(solution)/shard_map/jit(_solve_triangular)/vmap()/triangular_solve | solution.py:112
  411.6 16.0 %gather_fusion.4 = f32[2048,1025]{1,0:T(8,128)} fusion(f32[2049,1025]{1,0:T(8,128)} %pad.21, s32[2048]{0:T(1024)S(1)} %fusion.114), kind=kCustom, calls=%fused_computation.4 | custom fusion | bytes 16801792 | tf_op jit(solution)/shard_map/jit(_take)/gather | solution.py:212
  445.0 12.3 %gather_fusion.5 = f32[1024,2048]{1,0:T(8,128)} fusion(f32[2048,1025]{0,1:T(8,128)} %copy.100, s32[1024]{0:T(1024)S(1)} %fusion.126), kind=kCustom, calls=%fused_computation.5 | custom fusion | bytes 16781312 | tf_op jit(solution)/shard_map/jit(_take)/gather | solution.py:212
  466.5 12.2 %bitcast_add_fusion = f32[2048,1024]{1,0:T(8,128)} fusion(f32[2048,1024]{1,0:T(8,128)} %bitcast.171, f32[1024,2048]{0,1:T(8,128)} %copy.101, pred[1024]{0:T(1024)(128)(4,1)S(1)} %get-tuple-element.87), kind=kLoop, calls=%fused_computation.19 | loop fusion | flops 4194304 | bytes 25166848 | tf_op jit(solution)/shard_map/add | solution.py:213
  513.0 11.7 %cholesky.358 = f32[128,128]{1,0:T(8,128)S(1)} custom-call(f32[128,128]{1,0:T(8,128)S(1)} %cholesky.439), custom_call_target="Cholesky" | custom-call | tf_op jit(solution)/shard_map/jit(cholesky)/cholesky | solution.py:235
  538.7 12.1 %cholesky.377 = f32[128,128]{1,0:T(8,128)S(1)} custom-call(f32[128,128]{1,0:T(8,128)S(1)} %cholesky.443), custom_call_target="Cholesky" | custom-call | tf_op jit(solution)/shard_map/jit(cholesky)/cholesky | solution.py:235
  563.2 11.7 %cholesky.398 = f32[128,128]{1,0:T(8,128)S(1)} custom-call(f32[128,128]{1,0:T(8,128)S(1)} %cholesky.448), custom_call_target="Cholesky" | custom-call | tf_op jit(solution)/shard_map/jit(cholesky)/cholesky | solution.py:235
  574.9 10.0 %custom-call.37 = f32[1,128,128]{1,2,0:T(8,128)S(1)} custom-call(f32[1,128,128]{2,1,0:T(8,128)S(1)} %get-tuple-element.66), custom_call_target="InvertDiagBlocksLowerTriangular" | custom-call | tf_op jit(solution)/shard_map/jit(cholesky)/cholesky | solution.py:235
  586.3 11.7 %cholesky.415 = f32[128,128]{1,0:T(8,128)S(1)} custom-call(f32[128,128]{1,0:T(8,128)S(1)} %convolution_subtract_fusion.5), custom_call_target="Cholesky" | custom-call | tf_op jit(solution)/shard_map/jit(cholesky)/cholesky | solution.py:235
  606.1 39.9 %custom-call.38 = f32[4,1,128,128]{2,3,1,0:T(8,128)} custom-call(f32[4,1,128,128]{3,2,1,0:T(8,128)S(1)} %fusion.47), custom_call_target="InvertDiagBlocksLowerTriangular" | custom-call | tf_op jit(solution)/shard_map/jit(_solve_triangular)/vmap()/triangular_solve | solution.py:112
  654.8 30.1 %fusion.14 = f32[1024,1024]{1,0:T(8,128)} fusion(f32[1024,1024]{1,0:T(8,128)} %all-reduce.18.cloned.1.call-done, f32[512,512]{1,0:T(8,128)S(1)} %fusion.34, f32[512,512]{1,0:T(8,128)} %fusion.33, f32[512,512]{1,0:T(8,128)S(1)} %convolution_negate_fusion), kind=kOutput, calls=%fused_computation.47 | convolution fusion | flops 12889096192 | bytes 11534336 | tf_op jit(solution)/shard_map/dot_general | solution.py:246
  684.9 34.5 %all-reduce.16.cloned.1.call-done = f32[2048,1024]{1,0:T(8,128)} async-done(((f32[2048,1024]{1,0:T(8,128)}), f32[2048,1024]{1,0:T(8,128)}) %all-reduce.16.cloned.1.call-update) | async-done | bytes 8388624 | tf_op jit(solution)/shard_map/psum | solution.py:231
  719.4 30.4 %fusion.15 = f32[2048,1024]{1,0:T(8,128)S(1)} fusion(f32[2048,1024]{1,0:T(8,128)} %all-reduce.16.cloned.1.call-done, f32[512,512]{1,0:T(8,128)S(1)} %fusion.34, f32[512,512]{1,0:T(8,128)} %fusion.33, f32[512,512]{1,0:T(8,128)S(1)} %convolution_negate_fusion), kind=kOutput, calls=%fused_computation.48 | convolution fusion | flops 25773998080 | bytes 19922944 | tf_op jit(solution)/shard_map/dot_general | solution.py:245
  759.9 37.2 %fusion.1 = f32[2048,1024]{1,0:T(8,128)} fusion(f32[2048,512]{1,0:T(8,128)} %get-tuple-element.34, f32[2048,512]{1,0:T(8,128)} %get-tuple-element.33, f32[2048,1024]{1,0:T(8,128)S(1)} %bitcast.173, f32[1536,1024]{1,0:T(8,128)} %copy-done.1, f32[512,1024]{1,0:T(8,128)S(1)} %fusion.18, pred[]{:T(512)S(6)} %eq.118, pred[1024]{0:T(1024)(128)(4,1)S(1)} %copy-done.13, ...), kind=kOutput, calls=%fused_computation.18 | convolution fusion | flops 25789726720 | bytes 37761024 | tf_op jit(solution)/shard_map/dot_general | solution.py:256
  797.1 13.5 %reshape.749 = f32[4,1,512,2,1,512]{5,4,3,2,1,0:T(1,128)} reshape(f32[2048,1024]{1,0:T(8,128)} %fusion.1) | data formatting | bytes 16777216 | tf_op jit(solution)/shard_map/reshape | solution.py:260
  (251 shorter events, 269.1 us)
Async XLA Ops:
  9.3 11.7 %copy-start = (s32[8192]{0:T(1024)S(1)}, s32[8192]{0:T(1024)}, u32[]{:S(2)}) copy-start(s32[8192]{0:T(1024)} %param.8) | copy-start | bytes 98308
  53.7 1.6 copy-start.14
  62.6 73.1 %all-to-all-start = ((f32[1024,16,64]{0,2,1:T(8,128)}), f32[1024,16,64]{0,2,1:T(8,128)}, u32[]{:S(2)}, u32[]{:S(2)}) async-start(f32[1024,16,64]{0,2,1:T(8,128)} %bitcast.174), calls=%async_computation | async-start | bytes 8388608 | tf_op jit(solution)/shard_map/all_to_all | solution.py:202
  70.2 204.2 %all-reduce.14.cloned.1.call-start = ((), (), s32[]{:S(2)}) async-start(), calls=%async_computation.2 | async-start | bytes 8388608 | tf_op jit(solution)/shard_map/psum | solution.py:201
  124.9 276.5 %copy-start.8 = (f32[128,128]{1,0:T(8,128)}, f32[128,128]{1,0:T(8,128)S(1)}, u32[]{:S(2)}) copy-start(f32[128,128]{1,0:T(8,128)S(1)} %fusion.88) | copy-start | bytes 196612
  165.6 238.0 %all-to-all-start.1 = ((f32[8,256,1024]{2,1,0:T(8,128)}), f32[8,256,1024]{2,1,0:T(8,128)}, u32[]{:S(2)}, u32[]{:S(2)}) async-start(f32[8,256,1024]{2,1,0:T(8,128)} %broadcast_select_fusion.1), calls=%async_computation.1 | async-start | bytes 16777216 | tf_op jit(solution)/shard_map/all_to_all | solution.py:208
  173.7 481.1 %all-reduce.18.cloned.1.call-start = ((), (), s32[]{:S(2)}) async-start(), calls=%async_computation.4 | async-start | bytes 8388608 | tf_op jit(solution)/shard_map/psum | solution.py:232
  361.6 42.0 %copy-start.2 = (f32[512,512]{1,0:T(8,128)}, f32[512,512]{1,0:T(8,128)S(1)}, u32[]{:S(2)}) copy-start(f32[512,512]{1,0:T(8,128)S(1)} %select_select_fusion.1) | copy-start | bytes 3145732
  498.2 221.2 %all-reduce.16.cloned.1.call-start = ((), (), s32[]{:S(2)}) async-start(), calls=%async_computation.3 | async-start | bytes 16777216 | tf_op jit(solution)/shard_map/psum | solution.py:231
  511.9 1.0 copy-start.6
  538.0 0.7 copy-start.7
  538.7 107.3 %copy-start.9 = (f32[128,128]{1,0:T(8,128)S(1)}, f32[128,128]{1,0:T(8,128)}, u32[]{:S(2)}) copy-start(f32[128,128]{1,0:T(8,128)} %copy-done.8) | copy-start | bytes 196612
  602.6 1.5 copy-start.4
  749.8 1.2 copy-start.3
  749.8 1.5 copy-start.5
  751.4 7.2 copy-start.1
  751.4 7.2 slice-start
  752.6 7.3 slice-start.1
  752.6 7.3 copy-start.10
  752.6 7.3 copy-start.11
  752.6 7.3 copy-start.12
  752.6 7.3 copy-start.13
Sparse Core Ops, SparseCore 0:
  75.9 198.4 all-reduce.13
  498.3 74.5 all-reduce.17
  576.5 142.8 all-reduce.15

commit v8 on v6

--- a/solution.py
+++ b/solution.py
@@ -195,13 +195,14 @@
         child_to_parent, child_cblocks, grid_cols, block_width, my_col, cap_cols, local_cols
     )
     child_local = child_block.reshape(child_rows, child_cols)
+    d_part = corner_part(front, child_local, child_to_parent, my_row, my_col, grid_rows, grid_cols)
+    d_full = lax.psum(d_part, ("prow", "pcol"))
     staged = jnp.take(jnp.pad(child_local, ((0, 0), (0, 1))), col_send, axis=1)
     staged = lax.all_to_all(
         staged.reshape(child_rows, grid_cols, cap_cols), "pcol", split_axis=1, concat_axis=1, tiled=True
     ).reshape(child_rows, grid_cols * cap_cols)
     front_mat = front.reshape(local_rows, local_cols)
-    d_part = corner_part(front, child_local, child_to_parent, my_row, my_col, grid_rows, grid_cols)
-    staged, d_part, front_mat = lax.optimization_barrier((staged, d_part, front_mat))
+    staged, front_mat = lax.optimization_barrier((staged, front_mat))
     moved = jnp.take(jnp.pad(staged, ((0, 1), (0, 0))), row_send, axis=0)
     moved = lax.all_to_all(
         moved.reshape(grid_rows, cap_rows, grid_cols * cap_cols), "prow", split_axis=0, concat_axis=0, tiled=True
@@ -222,7 +223,6 @@
     y_part = jnp.concatenate(
         [jnp.where(my_row == p, first_rows, zero_rows) for p in range(NP)], axis=0
     )
-    d_full = lax.psum(d_part, ("prow", "pcol"))
     d_full, x_part, y_part = lax.optimization_barrier((d_full, x_part, y_part))
     x_full = lax.psum(x_part, "pcol")
     y_full = lax.psum(y_part, "prow")

time: 796 us -> 788 us (0.990)
    all_to_all x1, waiting for transfers between devices: 77.6 us -> 51 us  [local(): lax.all_to_all(moved.reshape(grid_rows, cap_rows, grid_cols * cap_cols),...]
    psum x1, waiting for transfers between devices: 13 us -> 26 us  [local(): d_full = lax.psum(d_part, ('prow', 'pcol'))]
  transfers between devices with their start and end apart: 5 -> 5, of which waited for: 2 -> 3; matrix products, arithmetic and copies ran while one was open for 55% -> 55% of each run, Pallas kernels for 0% -> 0%
where the time goes in v8:
time: 788 us; the launch traced here: 784 us
  other arithmetic  352 us (45%)
  local copies, waits for them, and re-layouts  174 us (22%)
  matrix products  139 us (18%)
  waiting for transfers between devices  84.2 us (11%)
  between operations  19.1 us (2%)
  starting transfers between devices  16.1 us (2%)
    another operation x32, other arithmetic, local(): low = jnp.tril(jnp.linalg.cholesky(d_full))  173 us
    another operation x2, other arithmetic, lower_inverse(): inv = jax.scipy.linalg.solve_triangular(diag, eye, lower=True)  78.8 us
    all_to_all x1, waiting for transfers between devices, local(): lax.all_to_all(moved.reshape(grid_rows, cap_rows, grid_cols * cap_cols),...  51 us
    gather x3, local copies, waits for them, and re-layouts, local(): added = jnp.take(jnp.take(arrived, row_recv, axis=0), col_recv, axis=1)  37.9 us
    dot_general x1, matrix products, local(): updated = matrix - jnp.dot(rows_u, cols_u.T, precision=HIGHEST)  37.2 us
    dot_general x1, matrix products, local(): rows_f = jnp.dot(x_full, low_inv.T, precision=HIGHEST)  30.1 us
    dot_general x1, matrix products, local(): lax.dot_general(y_full, low_inv, (((0,), (1,)), ((), ())), precision=HIGH...  29.7 us
    unnamed x4, other arithmetic  29.3 us
  transfers between devices with their start and end apart: 5, of which 3 were waited for; matrix products, arithmetic and copies ran while one was open for 55% of the time, Pallas kernels for 0%

profile of v8, /device:TPU:1, one launch (start us, length us, event | category | flops | bytes accessed | tf_op | source)
XLA Modules:
  0.0 783.7 jit_solution(12444825376874251988)
XLA Ops:
  36.0 29.2 %reduce.84 = f32[4,512,2,512]{3,2,1,0:T(2,128)} reduce(f32[4,1,512,2,1,512]{5,4,3,2,1,0:T(1,128)} %param.3, f32[]{:T(128)} %constant.627), dimensions={1,4}, to_apply=%param.3.reduce_sub_computation | reduce | bytes 16777220 | tf_op args[0]
  103.1 13.8 %gather_fusion.3 = f32[2048,1024]{1,0:T(8,128)} fusion(f32[1025,1024]{1,0:T(8,128)} %pad.17, s32[2048]{0:T(1024)S(1)} %broadcast_clamp_fusion), kind=kCustom, calls=%fused_computation.3 | custom fusion | bytes 16785408 | tf_op jit(solution)/shard_map/jit(_take)/gather | solution.py:206
  156.6 13.2 %gather_fusion.7 = s32[2048]{0:T(1024)S(1)} fusion(s32[8,1024]{1,0:T(8,128)S(1)} %bitcast.162, s32[2048]{0:T(1024)S(1)} %bitcast.163), kind=kCustom, calls=%fused_computation.7 | custom fusion | bytes 32768 | tf_op jit(solution)/shard_map/jit(take_along_axis)/gather | solution.py:55
  180.1 51.0 %all-to-all-done.1 = f32[8,256,1024]{2,1,0:T(8,128)} async-done(((f32[8,256,1024]{2,1,0:T(8,128)}), f32[8,256,1024]{2,1,0:T(8,128)}, u32[]{:S(2)}, u32[]{:S(2)}) %all-to-all-start.1) | async-done | bytes 8388640 | tf_op jit(solution)/shard_map/all_to_all | solution.py:207
  239.2 16.3 %gather_fusion.4 = f32[2048,1025]{1,0:T(8,128)} fusion(f32[2049,1025]{1,0:T(8,128)} %pad.18, s32[2048]{0:T(1024)S(1)} %fusion.115), kind=kCustom, calls=%fused_computation.4 | custom fusion | bytes 16801792 | tf_op jit(solution)/shard_map/jit(_take)/gather | solution.py:211
  273.0 12.3 %gather_fusion.5 = f32[1024,2048]{1,0:T(8,128)} fusion(f32[2048,1025]{0,1:T(8,128)} %copy.64, s32[1024]{0:T(1024)S(1)} %get-tuple-element.74), kind=kCustom, calls=%fused_computation.5 | custom fusion | bytes 16781312 | tf_op jit(solution)/shard_map/jit(_take)/gather | solution.py:211
  294.6 12.4 %bitcast_add_fusion = f32[2048,1024]{1,0:T(8,128)} fusion(f32[2048,1024]{1,0:T(8,128)} %bitcast.166, f32[1024,2048]{0,1:T(8,128)} %copy.65, pred[1024]{0:T(1024)(128)(4,1)S(1)} %compare_and_fusion.5), kind=kLoop, calls=%fused_computation.19 | loop fusion | flops 4194304 | bytes 25166848 | tf_op jit(solution)/shard_map/add | solution.py:212
  319.5 26.0 %all-reduce.11.cloned.1.call-done = f32[1024,1024]{0,1:T(8,128)} async-done(((f32[1024,1024]{0,1:T(8,128)}), f32[1024,1024]{0,1:T(8,128)}) %all-reduce.11.cloned.1.call-update) | async-done | bytes 4194320 | tf_op jit(solution)/shard_map/psum | solution.py:199
  357.6 11.7 %cholesky.228 = f32[128,128]{1,0:T(8,128)S(1)} custom-call(f32[128,128]{1,0:T(8,128)S(1)} %cholesky.589), custom_call_target="Cholesky" | custom-call | tf_op jit(solution)/shard_map/jit(cholesky)/cholesky | solution.py:229
  385.6 11.9 %cholesky.249 = f32[128,128]{1,0:T(8,128)S(1)} custom-call(f32[128,128]{1,0:T(8,128)S(1)} %cholesky.593), custom_call_target="Cholesky" | custom-call | tf_op jit(solution)/shard_map/jit(cholesky)/cholesky | solution.py:229
  411.3 11.7 %cholesky.478 = f32[128,128]{1,0:T(8,128)S(1)} custom-call(f32[128,128]{1,0:T(8,128)S(1)} %cholesky.598), custom_call_target="Cholesky" | custom-call | tf_op jit(solution)/shard_map/jit(cholesky)/cholesky | solution.py:229
  423.6 9.8 %custom-call.65 = f32[1,128,128]{1,2,0:T(8,128)S(1)} custom-call(f32[1,128,128]{2,1,0:T(8,128)S(1)} %get-tuple-element.60), custom_call_target="InvertDiagBlocksLowerTriangular" | custom-call | tf_op jit(solution)/shard_map/jit(cholesky)/cholesky | solution.py:229
  437.3 11.7 %cholesky.497 = f32[128,128]{1,0:T(8,128)S(1)} custom-call(f32[128,128]{1,0:T(8,128)S(1)} %cholesky.603), custom_call_target="Cholesky" | custom-call | tf_op jit(solution)/shard_map/jit(cholesky)/cholesky | solution.py:229
  449.6 9.8 %custom-call.66 = f32[1,128,128]{1,2,0:T(8,128)S(1)} custom-call(f32[1,128,128]{2,1,0:T(8,128)S(1)} %get-tuple-element.57), custom_call_target="InvertDiagBlocksLowerTriangular" | custom-call | tf_op jit(solution)/shard_map/jit(cholesky)/cholesky | solution.py:229
  462.9 12.1 %cholesky.516 = f32[128,128]{1,0:T(8,128)S(1)} custom-call(f32[128,128]{1,0:T(8,128)S(1)} %cholesky.608), custom_call_target="Cholesky" | custom-call | tf_op jit(solution)/shard_map/jit(cholesky)/cholesky | solution.py:229
  488.8 11.7 %cholesky.536 = f32[128,128]{1,0:T(8,128)S(1)} custom-call(f32[128,128]{1,0:T(8,128)S(1)} %cholesky.613), custom_call_target="Cholesky" | custom-call | tf_op jit(solution)/shard_map/jit(cholesky)/cholesky | solution.py:229
  501.1 9.8 %custom-call.68 = f32[1,128,128]{1,2,0:T(8,128)S(1)} custom-call(f32[1,128,128]{2,1,0:T(8,128)S(1)} %get-tuple-element.51), custom_call_target="InvertDiagBlocksLowerTriangular" | custom-call | tf_op jit(solution)/shard_map/jit(cholesky)/cholesky | solution.py:229
  514.0 11.9 %cholesky.556 = f32[128,128]{1,0:T(8,128)S(1)} custom-call(f32[128,128]{1,0:T(8,128)S(1)} %cholesky.618), custom_call_target="Cholesky" | custom-call | tf_op jit(solution)/shard_map/jit(cholesky)/cholesky | solution.py:229
  538.9 11.7 %cholesky.574 = f32[128,128]{1,0:T(8,128)S(1)} custom-call(f32[128,128]{1,0:T(8,128)S(1)} %convolution_subtract_fusion.6), custom_call_target="Cholesky" | custom-call | tf_op jit(solution)/shard_map/jit(cholesky)/cholesky | solution.py:229
  566.1 78.8 %custom-call.70 = f32[8,1,128,128]{2,3,1,0:T(8,128)S(1)} custom-call(f32[8,1,128,128]{3,2,1,0:T(8,128)S(1)} %broadcast_select_fusion.3), custom_call_target="InvertDiagBlocksLowerTriangular" | custom-call | tf_op jit(solution)/shard_map/jit(_solve_triangular)/vmap()/triangular_solve | solution.py:112
  655.8 29.7 %fusion.16 = f32[1024,1024]{1,0:T(8,128)} fusion(f32[1024,1024]{1,0:T(8,128)} %all-reduce.15.cloned.1.call-done, f32[1,512,512]{2,1,0:T(8,128)S(1)} %get-tuple-element.36, f32[1,512,512]{2,1,0:T(8,128)S(1)} %get-tuple-element.35, f32[1,512,512]{2,1,0:T(8,128)S(1)} %fusion.31), kind=kOutput, calls=%fused_computation.48 | convolution fusion | flops 12889096192 | bytes 11534336 | tf_op jit(solution)/shard_map/dot_general | solution.py:232
  685.4 30.1 %fusion.18 = f32[2048,1024]{1,0:T(8,128)S(1)} fusion(f32[2048,1024]{1,0:T(8,128)} %all-reduce.13.cloned.1.call-done, f32[1,512,512]{2,1,0:T(8,128)S(1)} %get-tuple-element.36, f32[1,512,512]{2,1,0:T(8,128)S(1)} %get-tuple-element.35, f32[1,512,512]{2,1,0:T(8,128)S(1)} %fusion.31), kind=kOutput, calls=%fused_computation.49 | convolution fusion | flops 25773998080 | bytes 19922944 | tf_op jit(solution)/shard_map/dot_general | solution.py:231
  726.3 37.2 %fusion.1 = f32[2048,1024]{1,0:T(8,128)} fusion(f32[2048,512]{1,0:T(8,128)} %get-tuple-element.24, f32[2048,512]{1,0:T(8,128)} %get-tuple-element.23, f32[2048,1024]{1,0:T(8,128)S(1)} %bitcast.168, f32[1536,1024]{1,0:T(8,128)} %copy-done.1, f32[512,1024]{1,0:T(8,128)S(1)} %slice_select_fusion.2, pred[]{:T(512)S(6)} %eq.114, ...), kind=kOutput, calls=%fused_computation.18 | convolution fusion | flops 25789726720 | bytes 37761024 | tf_op jit(solution)/shard_map/dot_general | solution.py:242
  763.5 13.5 %reshape.898 = f32[4,1,512,2,1,512]{5,4,3,2,1,0:T(1,128)} reshape(f32[2048,1024]{1,0:T(8,128)} %fusion.1) | data formatting | bytes 16777216 | tf_op jit(solution)/shard_map/reshape | solution.py:246
  (233 shorter events, 277.4 us)
Async XLA Ops:
  10.4 2.4 copy-start.5
  24.5 8.1 %copy-start = (s32[8192]{0:T(1024)S(1)}, s32[8192]{0:T(1024)}, u32[]{:S(2)}) copy-start(s32[8192]{0:T(1024)} %param.5) | copy-start | bytes 98308
  24.5 68.1 %all-to-all-start = ((f32[1024,16,64]{0,2,1:T(8,128)}), f32[1024,16,64]{0,2,1:T(8,128)}, u32[]{:S(2)}, u32[]{:S(2)}) async-start(f32[1024,16,64]{0,2,1:T(8,128)} %broadcast_select_fusion.2), calls=%async_computation | async-start | bytes 8388608 | tf_op jit(solution)/shard_map/all_to_all | solution.py:201
  122.8 108.3 %all-to-all-start.1 = ((f32[8,256,1024]{2,1,0:T(8,128)}), f32[8,256,1024]{2,1,0:T(8,128)}, u32[]{:S(2)}, u32[]{:S(2)}) async-start(f32[8,256,1024]{2,1,0:T(8,128)} %broadcast_select_fusion.1), calls=%async_computation.1 | async-start | bytes 16777216 | tf_op jit(solution)/shard_map/all_to_all | solution.py:207
  130.6 214.9 %all-reduce.11.cloned.1.call-start = ((), (), s32[]{:S(2)}) async-start(), calls=%async_computation.2 | async-start | bytes 8388608 | tf_op jit(solution)/shard_map/psum | solution.py:199
  133.3 11.8 %copy-start.6 = (f32[2,1,512,1,1,512]{5,2,3,4,1,0:T(8,128)S(1)}, f32[2,1,512,1,1,512]{5,2,3,4,1,0:T(8,128)}, u32[]{:S(2)}) copy-start(f32[2,1,512,1,1,512]{5,2,3,4,1,0:T(8,128)} %copy-done.5) | copy-start | bytes 6291460
  156.0 499.8 %all-reduce.15.cloned.1.call-start = ((), (), s32[]{:S(2)}) async-start(), calls=%async_computation.4 | async-start | bytes 8388608 | tf_op jit(solution)/shard_map/psum | solution.py:228
  355.6 2.0 copy-start.4
  433.5 252.0 %all-reduce.13.cloned.1.call-start = ((), (), s32[]{:S(2)}) async-start(), calls=%async_computation.3 | async-start | bytes 16777216 | tf_op jit(solution)/shard_map/psum | solution.py:227
  564.1 2.0 copy-start.2
  715.6 2.2 copy-start.3
  717.8 7.2 copy-start.1
  717.8 7.2 slice-start
  718.2 8.1 %slice-start.1 = ((s8[8388608]{0:T(1024)(128)(4,1)}), s8[4194304]{0:T(1024)(128)(4,1)S(1)}, s32[]{:S(2)}) async-start(s8[8388608]{0:T(1024)(128)(4,1)} %bitcast.167), calls=%async_computation.6 | async-start | bytes 8388608
Sparse Core Ops, SparseCore 0:
  156.1 189.3 all-reduce.10
  433.6 69.7 all-reduce.14
  512.0 139.4 all-reduce.12

commit v9 on v8

--- a/solution.py
+++ b/solution.py
@@ -196,7 +196,18 @@
     )
     child_local = child_block.reshape(child_rows, child_cols)
     d_part = corner_part(front, child_local, child_to_parent, my_row, my_col, grid_rows, grid_cols)
-    d_full = lax.psum(d_part, ("prow", "pcol"))
+    half = d_part.shape[0] // 2
+    d_low = lax.psum(
+        jnp.concatenate([d_part[:half, :half], d_part[half:, :half], d_part[half:, half:]], axis=0),
+        ("prow", "pcol"),
+    )
+    d_full = jnp.concatenate(
+        [
+            jnp.concatenate([d_low[:half], d_low[half : 2 * half].T], axis=1),
+            jnp.concatenate([d_low[half : 2 * half], d_low[2 * half :]], axis=1),
+        ],
+        axis=0,
+    )
     staged = jnp.take(jnp.pad(child_local, ((0, 0), (0, 1))), col_send, axis=1)
     staged = lax.all_to_all(
         staged.reshape(child_rows, grid_cols, cap_cols), "pcol", split_axis=1, concat_axis=1, tiled=True

time: 788 us -> 889 us (1.13)
  waiting for transfers between devices: 84.2 us -> 154 us
  other arithmetic: 352 us -> 378 us
    psum x1, waiting for transfers between devices: 26 us -> 154 us  [local(): lax.psum(jnp.concatenate([d_part[:half, :half], d_part[half:, :half], d_p...]
    all_to_all x1, waiting for transfers between devices: 51 us -> 0.01 us  [local(): lax.all_to_all(moved.reshape(grid_rows, cap_rows, grid_cols * cap_cols),...]
    another operation x2, other arithmetic: 9.52 us -> 21 us  [route_tables(): jnp.argmax(match, axis=1).astype(jnp.int32)]
    unnamed x34 -> x37, local copies, waits for them, and re-layouts: 21.6 us -> 22.9 us
  transfers between devices with their start and end apart: 5 -> 5, of which waited for: 3 -> 1; matrix products, arithmetic and copies ran while one was open for 55% -> 42% of each run, Pallas kernels for 0% -> 0%
where the time goes in v9:
time: 889 us; the launch traced here: 881 us
  other arithmetic  378 us (43%)
  local copies, waits for them, and re-layouts  180 us (20%)
  waiting for transfers between devices  154 us (17%)
  matrix products  135 us (15%)
  between operations  19.1 us (2%)
  starting transfers between devices  14.9 us (2%)
    another operation x32, other arithmetic, local(): low = jnp.tril(jnp.linalg.cholesky(d_full))  173 us
    psum x1, waiting for transfers between devices, local(): lax.psum(jnp.concatenate([d_part[:half, :half], d_part[half:, :half], d_p...  154 us
    another operation x2, other arithmetic, lower_inverse(): inv = jax.scipy.linalg.solve_triangular(diag, eye, lower=True)  79 us
    gather x3, local copies, waits for them, and re-layouts, local(): added = jnp.take(jnp.take(arrived, row_recv, axis=0), col_recv, axis=1)  37.6 us
    dot_general x1, matrix products, local(): updated = matrix - jnp.dot(rows_u, cols_u.T, precision=HIGHEST)  37.2 us
    dot_general x1, matrix products, local(): rows_f = jnp.dot(x_full, low_inv.T, precision=HIGHEST)  30.3 us
    dot_general x1, matrix products, local(): lax.dot_general(y_full, low_inv, (((0,), (1,)), ((), ())), precision=HIGH...  29.4 us
    unnamed x4, other arithmetic  29.3 us
  transfers between devices with their start and end apart: 5, of which 1 were waited for; matrix products, arithmetic and copies ran while one was open for 42% of the time, Pallas kernels for 0%

profile of v9, /device:TPU:1, one launch (start us, length us, event | category | flops | bytes accessed | tf_op | source)
XLA Modules:
  0.0 881.4 jit_solution(11524538988838124014)
XLA Ops:
  33.1 29.2 %reduce.84 = f32[4,512,2,512]{3,2,1,0:T(2,128)} reduce(f32[4,1,512,2,1,512]{5,4,3,2,1,0:T(1,128)} %param.3, f32[]{:T(128)} %constant.627), dimensions={1,4}, to_apply=%param.3.reduce_sub_computation | reduce | bytes 16777220 | tf_op args[0]
  82.9 13.4 %iota_reduce_fusion.1 = (pred[1024]{0:T(1024)(128)(4,1)}, s32[1024]{0:T(1024)S(1)}) fusion(s32[1024]{0:T(1024)S(1)} %fusion.119), kind=kLoop, calls=%fused_computation.40 | loop fusion | flops 8381440 | bytes 9216 | tf_op jit(solution)/shard_map/route_tables/reduce | solution.py:62
  106.5 13.8 %gather_fusion.3 = f32[2048,1024]{1,0:T(8,128)} fusion(f32[1025,1024]{1,0:T(8,128)} %pad.17, s32[2048]{0:T(1024)S(1)} %broadcast_clamp_fusion), kind=kCustom, calls=%fused_computation.3 | custom fusion | bytes 16785408 | tf_op jit(solution)/shard_map/jit(_take)/gather | solution.py:217
  157.8 13.0 %gather_fusion.7 = s32[2048]{0:T(1024)S(1)} fusion(s32[8,1024]{1,0:T(8,128)S(1)} %bitcast.164, s32[2048]{0:T(1024)S(1)} %bitcast.165), kind=kCustom, calls=%fused_computation.7 | custom fusion | bytes 32768 | tf_op jit(solution)/shard_map/jit(take_along_axis)/gather | solution.py:55
  181.4 154.0 %all-reduce.11.cloned.1.call-done = f32[1536,512]{0,1:T(8,128)} async-done(((f32[1536,512]{0,1:T(8,128)}), f32[1536,512]{0,1:T(8,128)}) %all-reduce.11.cloned.1.call-update) | async-done | bytes 3145744 | tf_op jit(solution)/shard_map/psum | solution.py:200
  356.7 16.1 %gather_fusion.4 = f32[2048,1025]{1,0:T(8,128)} fusion(f32[2049,1025]{1,0:T(8,128)} %pad.18, s32[2048]{0:T(1024)S(1)} %fusion.115), kind=kCustom, calls=%fused_computation.4 | custom fusion | bytes 16801792 | tf_op jit(solution)/shard_map/jit(_take)/gather | solution.py:222
  390.2 12.3 %gather_fusion.5 = f32[1024,2048]{1,0:T(8,128)} fusion(f32[2048,1025]{0,1:T(8,128)} %copy.72, s32[1024]{0:T(1024)S(1)} %get-tuple-element.78), kind=kCustom, calls=%fused_computation.5 | custom fusion | bytes 16781312 | tf_op jit(solution)/shard_map/jit(_take)/gather | solution.py:222
  411.7 12.2 %bitcast_add_fusion = f32[2048,1024]{1,0:T(8,128)} fusion(f32[2048,1024]{1,0:T(8,128)} %bitcast.168, f32[1024,2048]{0,1:T(8,128)} %copy.73, pred[1024]{0:T(1024)(128)(4,1)S(1)} %compare_and_fusion.5), kind=kLoop, calls=%fused_computation.19 | loop fusion | flops 4194304 | bytes 25166848 | tf_op jit(solution)/shard_map/add | solution.py:223
  455.2 11.7 %cholesky.228 = f32[128,128]{1,0:T(8,128)S(1)} custom-call(f32[128,128]{1,0:T(8,128)S(1)} %cholesky.589), custom_call_target="Cholesky" | custom-call | tf_op jit(solution)/shard_map/jit(cholesky)/cholesky | solution.py:240
  469.4 9.8 %custom-call.63 = f32[1,128,128]{1,2,0:T(8,128)S(1)} custom-call(f32[1,128,128]{2,1,0:T(8,128)S(1)} %get-tuple-element.70), custom_call_target="InvertDiagBlocksLowerTriangular" | custom-call | tf_op jit(solution)/shard_map/jit(cholesky)/cholesky | solution.py:240
  483.1 11.9 %cholesky.249 = f32[128,128]{1,0:T(8,128)S(1)} custom-call(f32[128,128]{1,0:T(8,128)S(1)} %cholesky.593), custom_call_target="Cholesky" | custom-call | tf_op jit(solution)/shard_map/jit(cholesky)/cholesky | solution.py:240
  495.6 9.8 %custom-call.64 = f32[1,128,128]{1,2,0:T(8,128)S(1)} custom-call(f32[1,128,128]{2,1,0:T(8,128)S(1)} %get-tuple-element.67), custom_call_target="InvertDiagBlocksLowerTriangular" | custom-call | tf_op jit(solution)/shard_map/jit(cholesky)/cholesky | solution.py:240
  508.8 11.7 %cholesky.478 = f32[128,128]{1,0:T(8,128)S(1)} custom-call(f32[128,128]{1,0:T(8,128)S(1)} %cholesky.598), custom_call_target="Cholesky" | custom-call | tf_op jit(solution)/shard_map/jit(cholesky)/cholesky | solution.py:240
  521.2 9.8 %custom-call.65 = f32[1,128,128]{1,2,0:T(8,128)S(1)} custom-call(f32[1,128,128]{2,1,0:T(8,128)S(1)} %get-tuple-element.64), custom_call_target="InvertDiagBlocksLowerTriangular" | custom-call | tf_op jit(solution)/shard_map/jit(cholesky)/cholesky | solution.py:240
  535.0 11.7 %cholesky.497 = f32[128,128]{1,0:T(8,128)S(1)} custom-call(f32[128,128]{1,0:T(8,128)S(1)} %cholesky.603), custom_call_target="Cholesky" | custom-call | tf_op jit(solution)/shard_map/jit(cholesky)/cholesky | solution.py:240
  560.6 11.8 %cholesky.516 = f32[128,128]{1,0:T(8,128)S(1)} custom-call(f32[128,128]{1,0:T(8,128)S(1)} %cholesky.608), custom_call_target="Cholesky" | custom-call | tf_op jit(solution)/shard_map/jit(cholesky)/cholesky | solution.py:240
  586.3 11.7 %cholesky.536 = f32[128,128]{1,0:T(8,128)S(1)} custom-call(f32[128,128]{1,0:T(8,128)S(1)} %cholesky.613), custom_call_target="Cholesky" | custom-call | tf_op jit(solution)/shard_map/jit(cholesky)/cholesky | solution.py:240
  611.5 11.9 %cholesky.556 = f32[128,128]{1,0:T(8,128)S(1)} custom-call(f32[128,128]{1,0:T(8,128)S(1)} %cholesky.618), custom_call_target="Cholesky" | custom-call | tf_op jit(solution)/shard_map/jit(cholesky)/cholesky | solution.py:240
  636.5 11.7 %cholesky.574 = f32[128,128]{1,0:T(8,128)S(1)} custom-call(f32[128,128]{1,0:T(8,128)S(1)} %convolution_subtract_fusion.6), custom_call_target="Cholesky" | custom-call | tf_op jit(solution)/shard_map/jit(cholesky)/cholesky | solution.py:240
  663.7 79.0 %custom-call.70 = f32[8,1,128,128]{2,3,1,0:T(8,128)S(1)} custom-call(f32[8,1,128,128]{3,2,1,0:T(8,128)S(1)} %broadcast_select_fusion.3), custom_call_target="InvertDiagBlocksLowerTriangular" | custom-call | tf_op jit(solution)/shard_map/jit(_solve_triangular)/vmap()/triangular_solve | solution.py:112
  753.6 29.4 %fusion.16 = f32[1024,1024]{1,0:T(8,128)} fusion(f32[1024,1024]{1,0:T(8,128)} %all-reduce.15.cloned.1.call-done, f32[1,512,512]{2,1,0:T(8,128)S(1)} %get-tuple-element.40, f32[1,512,512]{2,1,0:T(8,128)S(1)} %get-tuple-element.39, f32[1,512,512]{2,1,0:T(8,128)S(1)} %fusion.31), kind=kOutput, calls=%fused_computation.50 | convolution fusion | flops 12889096192 | bytes 11534336 | tf_op jit(solution)/shard_map/dot_general | solution.py:243
  783.0 30.3 %fusion.18 = f32[2048,1024]{1,0:T(8,128)S(1)} fusion(f32[2048,1024]{1,0:T(8,128)} %all-reduce.13.cloned.1.call-done, f32[1,512,512]{2,1,0:T(8,128)S(1)} %get-tuple-element.40, f32[1,512,512]{2,1,0:T(8,128)S(1)} %get-tuple-element.39, f32[1,512,512]{2,1,0:T(8,128)S(1)} %fusion.31), kind=kOutput, calls=%fused_computation.51 | convolution fusion | flops 25773998080 | bytes 19922944 | tf_op jit(solution)/shard_map/dot_general | solution.py:242
  824.0 37.2 %fusion.1 = f32[2048,1024]{1,0:T(8,128)} fusion(f32[2048,512]{1,0:T(8,128)} %get-tuple-element.24, f32[2048,512]{1,0:T(8,128)} %get-tuple-element.23, f32[2048,1024]{1,0:T(8,128)S(1)} %bitcast.170, f32[1536,1024]{1,0:T(8,128)} %copy-done.1, f32[512,1024]{1,0:T(8,128)S(1)} %slice_select_fusion.2, pred[]{:T(512)S(6)} %eq.114, ...), kind=kOutput, calls=%fused_computation.18 | convolution fusion | flops 25789726720 | bytes 37761024 | tf_op jit(solution)/shard_map/dot_general | solution.py:253
  861.2 13.5 %reshape.898 = f32[4,1,512,2,1,512]{5,4,3,2,1,0:T(1,128)} reshape(f32[2048,1024]{1,0:T(8,128)} %fusion.1) | data formatting | bytes 16777216 | tf_op jit(solution)/shard_map/reshape | solution.py:257
  (243 shorter events, 285.2 us)
Async XLA Ops:
  10.4 2.4 copy-start.5
  24.5 8.2 copy-start
  24.5 72.0 %all-to-all-start = ((f32[1024,16,64]{0,2,1:T(8,128)}), f32[1024,16,64]{0,2,1:T(8,128)}, u32[]{:S(2)}, u32[]{:S(2)}) async-start(f32[1024,16,64]{0,2,1:T(8,128)} %broadcast_select_fusion.2), calls=%async_computation | async-start | bytes 8388608 | tf_op jit(solution)/shard_map/all_to_all | solution.py:212
  126.2 222.4 %all-to-all-start.1 = ((f32[8,256,1024]{2,1,0:T(8,128)}), f32[8,256,1024]{2,1,0:T(8,128)}, u32[]{:S(2)}, u32[]{:S(2)}) async-start(f32[8,256,1024]{2,1,0:T(8,128)} %broadcast_select_fusion.1), calls=%async_computation.1 | async-start | bytes 16777216 | tf_op jit(solution)/shard_map/all_to_all | solution.py:218
  132.5 202.9 %all-reduce.11.cloned.1.call-start = ((), (), s32[]{:S(2)}) async-start(), calls=%async_computation.2 | async-start | bytes 6291456 | tf_op jit(solution)/shard_map/psum | solution.py:200
  135.5 11.8 %copy-start.6 = (f32[2,1,512,1,1,512]{5,2,3,4,1,0:T(8,128)S(1)}, f32[2,1,512,1,1,512]{5,2,3,4,1,0:T(8,128)}, u32[]{:S(2)}) copy-start(f32[2,1,512,1,1,512]{5,2,3,4,1,0:T(8,128)} %copy-done.5) | copy-start | bytes 6291460
  157.2 596.3 %all-reduce.15.cloned.1.call-start = ((), (), s32[]{:S(2)}) async-start(), calls=%async_computation.4 | async-start | bytes 8388608 | tf_op jit(solution)/shard_map/psum | solution.py:239
  341.9 2.3 copy-start.7
  453.2 2.0 copy-start.4
  531.0 252.0 %all-reduce.13.cloned.1.call-start = ((), (), s32[]{:S(2)}) async-start(), calls=%async_computation.3 | async-start | bytes 16777216 | tf_op jit(solution)/shard_map/psum | solution.py:238
  661.7 2.0 copy-start.2
  813.3 2.2 copy-start.3
  815.5 7.2 copy-start.1
  815.5 7.2 slice-start
  815.9 8.1 slice-start.1
Sparse Core Ops, SparseCore 0:
  157.3 178.0 all-reduce.10
  531.1 70.2 all-reduce.14
  609.5 139.9 all-reduce.12
